TPU v7x, 256 devices: a whole 4x4x8 slice. The times are simulated.
256 devices in a mesh: leaf: 4 (over z_hi), row: 8 (over z_lo, y), col: 8 (over x, core).
Axes of the slice: x: 4, y: 4, z: 8 (z_hi: 4, z_lo: 2; z = z_hi * 2 + z_lo), core: 2. Of those that a mesh axis runs over, the one named last changes fastest.
Arguments:
- lanczos_low: float32 [4, 8, 8, 128, 256], P('leaf', 'col', 'row'), may hold values from -6 to 6
- lanczos_mid: float32 [4, 8, 8, 96, 256], P('leaf', 'col', 'row'), may hold values from -6 to 6
- lanczos_top: float32 [4, 8, 8, 64, 256], P('leaf', 'col', 'row'), may hold values from -6 to 6
- pivot_low: bfloat16 [4, 8192, 8192], P('leaf', 'row', 'col'), as said below
- update_low: bfloat16 [4, 8192, 8192], P('leaf', 'row', 'col'), may hold values from -0.0625 to 0.0625
- pivot_mid: bfloat16 [12288, 24576], P('row', ('leaf', 'col'))
- update_mid: bfloat16 [12288, 16384], P('row', ('leaf', 'col')), may hold values from -0.0546875 to 0.0546875
- pivot_top: bfloat16 [16384, 16384], P('row', ('leaf', 'col'))
- rows_low: int32 [4, 8, 8, 2, 64], P('leaf', 'col', 'row'), may hold values from 0 to 20479, as said below
- rows_mid: int32 [4, 8, 8, 4, 16], P('leaf', 'col', 'row'), may hold values from 0 to 16383, as said below
Outputs:
- solved_low: float32 [4, 8, 8, 128, 256], P('leaf', 'col', 'row')
- solved_mid: float32 [4, 8, 8, 96, 256], P('leaf', 'col', 'row')
- solved_top: float32 [4, 8, 8, 64, 256], P('leaf', 'col', 'row')
Inputs may be any that keep to these rules, and one draw needn't show every extreme that they name: rows_low[2h + a, c, r, s, t] over t are distinct rows of front h, all among pivot rows a 6144 + (c * 8 + r) * 96 + k (0 <= k < 96) and update rows 12288 + a 4096 + (c * 8 + r) * 64 + k (0 <= k < 64); for s = 0 they include the first of those pivot rows and the last of those update rows. rows_mid[q, c, r, 2h + s, t] over s and t are distinct root rows q * 4096 + (c * 8 + r) * 64 + k (0 <= k < 64); for h = 0 they include the first and the last of them. pivot_low, pivot_mid's two square halves and pivot_top are lower triangular.
All inputs are finite; a program needn't handle non-finite values.
Results may differ from a plain program's by a relative error of at most 0.023.
Values may be sent and summed in bfloat16 or wider, within the bound.
No kernel may reach another device: no remote copies, remote signals or barrier semaphores. Data moves between devices by JAX's collectives and lax.ppermute only.
A program may use at most 64 MiB of HBM per device.

v0:
```python
import jax
import jax.numpy as jnp
from jax import lax
from jax.sharding import PartitionSpec as P

P1 = 12288


def from_partner(block, axis, bit):
    count = lax.axis_size(axis)
    route = []
    for low in range(count):
        high = low | 1 << bit
        if high != low and high < count:
            route += [(low, high), (high, low)]
    return lax.ppermute(block, axis, route)


def partner(block_data, leaf_bit):
    return from_partner(block_data.astype(jnp.bfloat16), "leaf", leaf_bit).astype(block_data.dtype)


def forward_apply(matrix, vector, leaf_bits):
    gathered = lax.all_gather(vector, "row", axis=0, tiled=True)
    result = lax.psum_scatter(
        jnp.dot(matrix, gathered, preferred_element_type=jnp.float32),
        "col",
        scatter_dimension=0,
        tiled=True,
    )
    for leaf_bit in leaf_bits:
        result = result + partner(result, leaf_bit)
    return result


def reverse_apply(matrix, vector):
    gathered = lax.all_gather(vector, "col", axis=0, tiled=True)
    return lax.psum_scatter(
        lax.dot_general(
            matrix, gathered, (((0,), (0,)), ((), ())), preferred_element_type=jnp.float32
        ).astype(jnp.bfloat16),
        "row",
        scatter_dimension=0,
        tiled=True,
    ).astype(jnp.float32)


def parent_slot(parent_rows, pivot_local, update_local):
    return jnp.where(
        parent_rows < P1, parent_rows % pivot_local, pivot_local + (parent_rows - P1) % update_local
    )


def pick_span(spans, index_value):
    return lax.dynamic_index_in_dim(spans, index_value, 0, keepdims=False)


def body(
    lanczos_low,
    lanczos_mid,
    lanczos_top,
    pivot_low,
    update_low,
    pivot_mid,
    update_mid,
    pivot_top,
    rows_low,
    rows_mid,
):
    rhs_width = lanczos_low.shape[-1]
    low_in = lanczos_low.reshape(-1, rhs_width)
    mid_in = lanczos_mid.reshape(-1, rhs_width)
    top_in = lanczos_top.reshape(-1, rhs_width)
    pivot_local_low = pivot_low[0]
    update_local_low = update_low[0]
    pivot_local = mid_in.shape[0]
    update_local = update_mid.shape[1] // lax.axis_size("row")
    top_local = top_in.shape[0]
    group_id = lax.axis_index("leaf")
    own_half = group_id % 2
    child_slots = parent_slot(rows_low.reshape(2, -1), pivot_local, update_local)
    root_slots = rows_mid.reshape(4, -1) % top_local
    source_order = jnp.bitwise_xor(group_id, jnp.arange(4, dtype=jnp.int32))
    source_slots = jnp.take(root_slots, source_order, axis=0).reshape(-1)
    own_slots = pick_span(child_slots, own_half)
    other_slots = pick_span(child_slots, 1 - own_half)
    low_y = forward_apply(pivot_local_low, low_in.astype(jnp.bfloat16), ())
    low_c = reverse_apply(update_local_low, low_y.astype(jnp.bfloat16)).reshape(2, -1, rhs_width)
    own_part = pick_span(low_c, own_half)
    came_part = partner(pick_span(low_c, 1 - own_half), 0)
    front_rows = jnp.concatenate([mid_in, jnp.zeros((update_local, rhs_width), mid_in.dtype)], 0)
    front_rows = front_rows.at[own_slots].add(-own_part).at[other_slots].add(-came_part)
    mid_y = forward_apply(pivot_mid, front_rows[:pivot_local].astype(jnp.bfloat16), (0,))
    mid_c = front_rows[pivot_local:] - reverse_apply(update_mid, mid_y.astype(jnp.bfloat16))
    spans = mid_c.reshape(4, -1, rhs_width)
    kept_spans = jnp.stack(
        [pick_span(spans, group_id), pick_span(spans, jnp.bitwise_xor(group_id, 2))]
    )
    moved_spans = partner(
        jnp.stack(
            [
                pick_span(spans, jnp.bitwise_xor(group_id, 1)),
                pick_span(spans, jnp.bitwise_xor(group_id, 3)),
            ]
        ),
        0,
    )
    second = partner(jnp.stack([kept_spans[1], moved_spans[1]]), 1)
    arrived = jnp.stack([kept_spans[0], moved_spans[0], second[0], second[1]]).reshape(
        -1, rhs_width
    )
    top_front = top_in.at[source_slots].add(arrived)
    top_y = forward_apply(pivot_top, top_front.astype(jnp.bfloat16), (0, 1))
    top_x = reverse_apply(pivot_top, top_y.astype(jnp.bfloat16))
    asked_rows = top_x[source_slots].reshape(4, -1, rhs_width)
    back_one = partner(jnp.stack([asked_rows[2], asked_rows[3]]), 1)
    back_zero = partner(jnp.stack([asked_rows[1], back_one[1]]), 0)
    by_root = jnp.stack([asked_rows[0], back_zero[0], back_one[0], back_zero[1]])
    mid_above = jnp.take(by_root, source_order, axis=0).reshape(-1, rhs_width)
    mid_sum = forward_apply(update_mid, mid_above.astype(jnp.bfloat16), (0,))
    mid_x = reverse_apply(pivot_mid, (mid_y - mid_sum).astype(jnp.bfloat16))
    front_values = jnp.concatenate([mid_x, mid_above], 0)
    own_rows = front_values[own_slots]
    got_rows = partner(front_values[other_slots], 0)
    low_above = jnp.where(
        own_half == 0,
        jnp.concatenate([own_rows, got_rows], 0),
        jnp.concatenate([got_rows, own_rows], 0),
    )
    low_sum = forward_apply(update_local_low, low_above.astype(jnp.bfloat16), ())
    low_x = reverse_apply(pivot_local_low, (low_y - low_sum).astype(jnp.bfloat16))
    return (
        low_x.reshape(lanczos_low.shape),
        mid_x.reshape(lanczos_mid.shape),
        top_x.reshape(lanczos_top.shape),
    )


def solution(mesh):
    return jax.shard_map(
        body,
        mesh=mesh,
        in_specs=(
            P("leaf", "col", "row", None, None),
            P("leaf", "col", "row", None, None),
            P("leaf", "col", "row", None, None),
            P("leaf", "row", "col"),
            P("leaf", "row", "col"),
            P("row", ("leaf", "col")),
            P("row", ("leaf", "col")),
            P("row", ("leaf", "col")),
            P("leaf", "col", "row", None, None),
            P("leaf", "col", "row", None, None),
        ),
        out_specs=(
            P("leaf", "col", "row", None, None),
            P("leaf", "col", "row", None, None),
            P("leaf", "col", "row", None, None),
        ),
        check_vma=False,
    )
```

profile of v0, /device:TPU:2, one launch (start us, length us, event | category | flops | bytes accessed | tf_op | source)
XLA Modules:
  0.0 739.1 jit_solution(14551251856389087296)
XLA Ops:
  7.2 1.1 convert_element_type.123
  8.3 29.8 %all-gather = bf16[1,1,1,1024,256]{4,3,2,1,0:T(8,128)(2,1)S(1)} all-gather(bf16[1,1,1,128,256]{4,3,2,1,0:T(8,128)(2,1)S(1)} %convert_element_type.123), channel_id=2, replica_groups=mesh['leaf'=4,'row'=8,'col'=8] {'row'}, dimensions={3}, use_global_device_ids=true | all-gather | bytes 589824 | tf_op jit(solution)/shard_map/all_gather | solution.py:24
  38.1 3.3 fusion.6
  41.5 33.6 %reduce-scatter.25.cloned.1.call-done = f32[128,256]{1,0:T(8,128)} async-done(((f32[1024,256]{1,0:T(8,128)}), f32[128,256]{1,0:T(8,128)}) %reduce-scatter.25.cloned.1.call-update) | async-done | bytes 131088 | tf_op jit(solution)/shard_map/reduce_scatter | solution.py:25
  76.0 13.8 %all_gather.31 = bf16[1024,256]{1,0:T(8,128)(2,1)S(1)} all-gather(bf16[128,256]{1,0:T(8,128)(2,1)S(1)} %convert_element_type.125), channel_id=1, replica_groups=mesh['leaf'=4,'row'=8,'col'=8] {'col'}, dimensions={0}, use_global_device_ids=true | all-gather | bytes 589824 | tf_op jit(solution)/shard_map/all_gather | solution.py:37
  89.8 2.3 fusion.17
  92.1 1.0 copy.43
  93.3 42.9 %reduce-scatter.31.cloned.1.call-done = bf16[128,256]{1,0:T(8,128)(2,1)} async-done(((bf16[1024,256]{1,0:T(8,128)(2,1)}), bf16[128,256]{1,0:T(8,128)(2,1)}) %reduce-scatter.31.cloned.1.call-update) | async-done | bytes 65552 | tf_op jit(solution)/shard_map/reduce_scatter | solution.py:38
  137.1 2.8 collective-permute-start
  139.9 1.0 scatter_custom_fusion
  140.9 1.4 collective-permute-done
  142.3 1.0 scatter_custom_fusion.1
  143.3 28.8 %all_gather.32 = bf16[768,256]{1,0:T(8,128)(2,1)S(1)} all-gather(bf16[96,256]{1,0:T(8,128)(2,1)S(1)} %slice.113), channel_id=1, replica_groups=mesh['leaf'=4,'row'=8,'col'=8] {'row'}, dimensions={0}, use_global_device_ids=true | all-gather | bytes 442368 | tf_op jit(solution)/shard_map/all_gather | solution.py:24
  172.2 2.0 convolution_bitcast_fusion.2
  174.1 3.0 copy.45
  177.3 31.0 %reduce-scatter.33.cloned.1.call-done = f32[192,256]{1,0:T(8,128)} async-done(((f32[1536,256]{1,0:T(8,128)}), f32[192,256]{1,0:T(8,128)}) %reduce-scatter.33.cloned.1.call-update) | async-done | bytes 196624
  208.3 1.1 copy.46
  209.3 2.6 collective-permute-start.1
  212.0 5.8 collective-permute-done.1
  217.9 14.6 %all_gather.33 = bf16[1536,256]{1,0:T(8,128)(2,1)S(1)} all-gather(bf16[192,256]{1,0:T(8,128)(2,1)S(1)} %copy.35), channel_id=1, replica_groups=mesh['leaf'=4,'row'=8,'col'=8] {'col'}, dimensions={0}, use_global_device_ids=true | all-gather | bytes 884736 | tf_op jit(solution)/shard_map/all_gather | solution.py:37
  232.5 2.0 fusion.24
  236.2 41.2 %reduce-scatter.35.cloned.1.call-done = bf16[64,256]{1,0:T(8,128)(2,1)} async-done(((bf16[512,256]{1,0:T(8,128)(2,1)}), bf16[64,256]{1,0:T(8,128)(2,1)}) %reduce-scatter.35.cloned.1.call-update) | async-done | bytes 32784 | tf_op jit(solution)/shard_map/reduce_scatter | solution.py:38
  278.2 2.6 collective-permute-start.2
  280.8 2.2 collective-permute-done.2
  283.0 4.8 collective-permute-start.3
  287.8 2.9 collective-permute-done.3
  290.7 1.0 scatter_fusion
  291.8 28.4 %all_gather.34 = bf16[512,256]{1,0:T(8,128)(2,1)S(1)} all-gather(bf16[64,256]{1,0:T(8,128)(2,1)S(1)} %convert_element_type.138), channel_id=1, replica_groups=mesh['leaf'=4,'row'=8,'col'=8] {'row'}, dimensions={0}, use_global_device_ids=true | all-gather | bytes 294912 | tf_op jit(solution)/shard_map/all_gather | solution.py:24
  320.1 3.7 convolution_bitcast_fusion.1
  323.9 32.4 %reduce-scatter.27.cloned.1.call-done = f32[256,256]{0,1:T(8,128)} async-done(((f32[2048,256]{0,1:T(8,128)}), f32[256,256]{0,1:T(8,128)}) %reduce-scatter.27.cloned.1.call-update) | async-done | bytes 262160 | tf_op jit(solution)/shard_map/reduce_scatter | solution.py:25
  356.3 1.0 convert_element_type.139
  357.2 2.7 collective-permute-start.4
  359.9 5.9 collective-permute-done.4
  365.8 1.0 fusion.28
  366.8 5.9 collective-permute-start.5
  372.7 6.4 collective-permute-done.5
  379.1 1.6 add_convert_fusion
  380.8 25.4 %all-gather.3.cloned.1.call-done = bf16[2048,256]{0,1:T(8,128)(2,1)} async-done(((bf16[256,256]{0,1:T(8,128)(2,1)}), bf16[2048,256]{0,1:T(8,128)(2,1)}) %all-gather.3.cloned.1.call-update) | async-done | bytes 1048592 | tf_op jit(solution)/shard_map/all_gather | solution.py:37
  406.2 2.6 fusion.25
  409.8 41.9 %reduce-scatter.37.cloned.1.call-done = bf16[64,256]{1,0:T(8,128)(2,1)} async-done(((bf16[512,256]{1,0:T(8,128)(2,1)}), bf16[64,256]{1,0:T(8,128)(2,1)}) %reduce-scatter.37.cloned.1.call-update) | async-done | bytes 32784 | tf_op jit(solution)/shard_map/reduce_scatter | solution.py:38
  451.7 1.4 gather_fusion.1
  453.1 5.1 collective-permute-start.6
  458.3 2.8 collective-permute-done.6
  461.1 2.5 collective-permute-start.7
  463.8 2.0 collective-permute-done.7
  466.4 28.4 %all_gather.36 = bf16[512,256]{1,0:T(8,128)(2,1)S(1)} all-gather(bf16[64,256]{1,0:T(8,128)(2,1)S(1)} %bitcast_select_fusion), channel_id=1, replica_groups=mesh['leaf'=4,'row'=8,'col'=8] {'row'}, dimensions={0}, use_global_device_ids=true | all-gather | bytes 294912 | tf_op jit(solution)/shard_map/all_gather | solution.py:24
  494.8 3.2 convolution_bitcast_fusion
  498.0 3.0 copy.51
  501.1 31.2 %reduce-scatter.39.cloned.1.call-done = f32[192,256]{1,0:T(8,128)} async-done(((f32[1536,256]{1,0:T(8,128)}), f32[192,256]{1,0:T(8,128)}) %reduce-scatter.39.cloned.1.call-update) | async-done | bytes 196624
  532.3 1.1 copy.52
  533.4 2.6 collective-permute-start.8
  536.0 5.8 collective-permute-done.8
  541.9 14.6 %all_gather.37 = bf16[1536,256]{1,0:T(8,128)(2,1)S(1)} all-gather(bf16[192,256]{1,0:T(8,128)(2,1)S(1)} %copy.38), channel_id=1, replica_groups=mesh['leaf'=4,'row'=8,'col'=8] {'col'}, dimensions={0}, use_global_device_ids=true | all-gather | bytes 884736 | tf_op jit(solution)/shard_map/all_gather | solution.py:37
  558.4 42.1 %reduce-scatter.41.cloned.1.call-done = bf16[96,256]{1,0:T(8,128)(2,1)} async-done(((bf16[768,256]{1,0:T(8,128)(2,1)}), bf16[96,256]{1,0:T(8,128)(2,1)}) %reduce-scatter.41.cloned.1.call-update) | async-done | bytes 49168 | tf_op jit(solution)/shard_map/reduce_scatter | solution.py:38
  601.9 2.6 collective-permute-start.9
  605.2 1.8 collective-permute-done.9
  607.1 29.0 %all_gather.38 = bf16[1024,256]{1,0:T(8,128)(2,1)S(1)} all-gather(bf16[128,256]{1,0:T(8,128)(2,1)S(1)} %fusion.29), channel_id=1, replica_groups=mesh['leaf'=4,'row'=8,'col'=8] {'row'}, dimensions={0}, use_global_device_ids=true | all-gather | bytes 589824 | tf_op jit(solution)/shard_map/all_gather | solution.py:24
  636.1 3.3 fusion.8
  639.5 30.3 %reduce-scatter.29.cloned.1.call-done = f32[128,256]{1,0:T(8,128)} async-done(((f32[1024,256]{1,0:T(8,128)}), f32[128,256]{1,0:T(8,128)}) %reduce-scatter.29.cloned.1.call-update) | async-done | bytes 131088 | tf_op jit(solution)/shard_map/reduce_scatter | solution.py:25
  670.6 13.7 %all_gather.39 = bf16[1024,256]{1,0:T(8,128)(2,1)S(1)} all-gather(bf16[128,256]{1,0:T(8,128)(2,1)S(1)} %subtract_convert_fusion.1), channel_id=1, replica_groups=mesh['leaf'=4,'row'=8,'col'=8] {'col'}, dimensions={0}, use_global_device_ids=true | all-gather | bytes 589824 | tf_op jit(solution)/shard_map/all_gather | solution.py:37
  684.4 2.3 fusion.20
  686.7 1.0 copy.55
  689.0 41.8 %reduce-scatter.43.cloned.1.call-done = bf16[128,256]{1,0:T(8,128)(2,1)} async-done(((bf16[1024,256]{1,0:T(8,128)(2,1)}), bf16[128,256]{1,0:T(8,128)(2,1)}) %reduce-scatter.43.cloned.1.call-update) | async-done | bytes 65552
  730.8 0.9 copy.56
  (94 shorter events, 13.8 us)
Async XLA Ops:
  7.2 165.0 %copy-start = (bf16[1536,768]{1,0:T(8,128)(2,1)S(1)}, bf16[1536,768]{1,0:T(8,128)(2,1)}, u32[]{:S(2)}) copy-start(bf16[1536,768]{1,0:T(8,128)(2,1)} %param.15) | copy-start | bytes 7077892
  7.2 67.9 %reduce-scatter.25.cloned.1.call-start = ((), (), s32[]{:S(2)}) async-start(), calls=%async_computation.10 | async-start | bytes 1179648 | tf_op jit(solution)/shard_map/reduce_scatter | solution.py:25
  41.4 94.8 %reduce-scatter.31.cloned.1.call-start = ((), (), s32[]{:S(2)}) async-start(), calls=%async_computation.14 | async-start | bytes 589824 | tf_op jit(solution)/shard_map/reduce_scatter | solution.py:38
  89.8 3.5 copy-start.7
  89.8 50.1 %copy-start.5 = (f32[1,1,1,96,256]{4,3,2,1,0:T(8,128)S(1)}, f32[1,1,1,96,256]{4,3,2,1,0:T(8,128)}, u32[]{:S(2)}) copy-start(f32[1,1,1,96,256]{4,3,2,1,0:T(8,128)} %param.11) | copy-start | bytes 294916
  93.2 115.1 %reduce-scatter.33.cloned.1.call-start = ((), (), s32[]{:S(2)}) async-start(), calls=%async_computation.15 | async-start | bytes 1769472
  137.1 5.2 collective-permute-start
  177.2 100.2 %reduce-scatter.35.cloned.1.call-start = ((), (), s32[]{:S(2)}) async-start(), calls=%async_computation.16 | async-start | bytes 294912 | tf_op jit(solution)/shard_map/reduce_scatter | solution.py:38
  209.3 8.4 %collective-permute-start.1 = (bf16[192,256]{0,1:T(8,128)(2,1)S(1)}, bf16[192,256]{0,1:T(8,128)(2,1)S(1)}, u32[]{:S(2)}, u32[]{:S(2)}) collective-permute-start(bf16[192,256]{0,1:T(8,128)(2,1)S(1)} %convert_element_type.131), channel_id=1, source_target_pairs={{0,64},{64,0},{128,192},{192,128},{1,65},{65,1},{129,193},{193,129... | collective-permute-start | bytes 294920 | tf_op jit(solution)/shard_map/ppermute | solution.py:16
  217.9 17.6 %copy-start.6 = (s32[1,1,1,4,16]{4,3,2,1,0:T(4,128)S(1)}, s32[1,1,1,4,16]{4,3,2,1,0:T(4,128)}, u32[]{:S(2)}) copy-start(s32[1,1,1,4,16]{4,3,2,1,0:T(4,128)} %param.19) | copy-start | bytes 772
  232.5 58.2 %copy-start.1 = (f32[1,1,1,64,256]{4,3,2,1,0:T(8,128)S(1)}, f32[1,1,1,64,256]{4,3,2,1,0:T(8,128)}, u32[]{:S(2)}) copy-start(f32[1,1,1,64,256]{4,3,2,1,0:T(8,128)} %param.12) | copy-start | bytes 196612
  235.4 120.9 %reduce-scatter.27.cloned.1.call-start = ((), (), s32[]{:S(2)}) async-start(), calls=%async_computation.11 | async-start | bytes 2359296 | tf_op jit(solution)/shard_map/reduce_scatter | solution.py:25
  278.2 4.8 collective-permute-start.2
  283.0 7.7 %collective-permute-start.3 = (bf16[2,16,256]{2,1,0:T(8,128)(2,1)S(1)}, bf16[2,16,256]{2,1,0:T(8,128)(2,1)S(1)}, u32[]{:S(2)}, u32[]{:S(2)}) collective-permute-start(bf16[2,16,256]{2,1,0:T(8,128)(2,1)S(1)} %pad_maximum_fusion.4), channel_id=1, source_target_pairs={{0,128},{128,0},{64,192},{192,64},{1,129},{129,1},{65,193},{193,65... | collective-permute-start | bytes 49160 | tf_op jit(solution)/shard_map/ppermute | solution.py:16
  323.9 82.4 %all-gather.3.cloned.1.call-start = ((), (), s32[]{:S(2)}) async-start(), calls=%async_computation.12 | async-start | bytes 1179648 | tf_op jit(solution)/shard_map/all_gather | solution.py:37
  357.2 8.6 %collective-permute-start.4 = (bf16[256,256]{0,1:T(8,128)(2,1)S(1)}, bf16[256,256]{0,1:T(8,128)(2,1)S(1)}, u32[]{:S(2)}, u32[]{:S(2)}) collective-permute-start(bf16[256,256]{0,1:T(8,128)(2,1)S(1)} %convert_element_type.139), channel_id=1, source_target_pairs={{0,64},{64,0},{128,192},{192,128},{1,65},{65,1},{129,193},{193,129... | collective-permute-start | bytes 393224 | tf_op jit(solution)/shard_map/ppermute | solution.py:16
  366.8 12.3 %collective-permute-start.5 = (bf16[256,256]{0,1:T(8,128)(2,1)S(1)}, bf16[256,256]{0,1:T(8,128)(2,1)S(1)}, u32[]{:S(2)}, u32[]{:S(2)}) collective-permute-start(bf16[256,256]{0,1:T(8,128)(2,1)S(1)} %fusion.28), channel_id=1, source_target_pairs={{0,128},{128,0},{64,192},{192,64},{1,129},{129,1},{65,193},{193,65... | collective-permute-start | bytes 393224 | tf_op jit(solution)/shard_map/ppermute | solution.py:16
  380.7 71.0 %reduce-scatter.37.cloned.1.call-start = ((), (), s32[]{:S(2)}) async-start(), calls=%async_computation.17 | async-start | bytes 294912 | tf_op jit(solution)/shard_map/reduce_scatter | solution.py:38
  409.7 122.6 %reduce-scatter.39.cloned.1.call-start = ((), (), s32[]{:S(2)}) async-start(), calls=%async_computation.18 | async-start | bytes 1769472
  453.1 7.9 %collective-permute-start.6 = (bf16[2,16,256]{2,1,0:T(8,128)(2,1)S(1)}, bf16[2,16,256]{2,1,0:T(8,128)(2,1)S(1)}, u32[]{:S(2)}, u32[]{:S(2)}) collective-permute-start(bf16[2,16,256]{2,1,0:T(8,128)(2,1)S(1)} %pad_maximum_fusion.5), channel_id=1, source_target_pairs={{0,128},{128,0},{64,192},{192,64},{1,129},{129,1},{65,193},{193,65... | collective-permute-start | bytes 49160 | tf_op jit(solution)/shard_map/ppermute | solution.py:16
  461.1 4.7 collective-permute-start.7
  501.1 99.4 %reduce-scatter.41.cloned.1.call-start = ((), (), s32[]{:S(2)}) async-start(), calls=%async_computation.19 | async-start | bytes 442368 | tf_op jit(solution)/shard_map/reduce_scatter | solution.py:38
  533.4 8.4 %collective-permute-start.8 = (bf16[192,256]{0,1:T(8,128)(2,1)S(1)}, bf16[192,256]{0,1:T(8,128)(2,1)S(1)}, u32[]{:S(2)}, u32[]{:S(2)}) collective-permute-start(bf16[192,256]{0,1:T(8,128)(2,1)S(1)} %convert_element_type.149), channel_id=1, source_target_pairs={{0,64},{64,0},{128,192},{192,128},{1,65},{65,1},{129,193},{193,129... | collective-permute-start | bytes 294920 | tf_op jit(solution)/shard_map/ppermute | solution.py:16
  558.3 111.4 %reduce-scatter.29.cloned.1.call-start = ((), (), s32[]{:S(2)}) async-start(), calls=%async_computation.13 | async-start | bytes 1179648 | tf_op jit(solution)/shard_map/reduce_scatter | solution.py:25
  601.9 5.1 collective-permute-start.9
  636.1 33.7 %copy-start.3 = (f32[128,256]{1,0:T(8,128)S(1)}, f32[128,256]{1,0:T(8,128)}, u32[]{:S(2)}) copy-start(f32[128,256]{1,0:T(8,128)} %reduce-scatter.25.cloned.1.call-done) | copy-start | bytes 393220
  639.4 91.4 %reduce-scatter.43.cloned.1.call-start = ((), (), s32[]{:S(2)}) async-start(), calls=%async_computation.20 | async-start | bytes 589824
  684.4 3.4 copy-start.2
  684.4 4.0 copy-start.4
Sparse Core Ops, SparseCore 0:
  41.6 33.4 reduce-scatter.24
  93.3 42.8 reduce-scatter.30
  177.3 30.8 reduce-scatter.32
  235.5 41.8 reduce-scatter.34
  324.0 32.2 reduce-scatter.26
  380.9 25.3 all-gather.2
  409.8 41.8 reduce-scatter.36
  501.2 31.0 reduce-scatter.38
  558.4 41.9 reduce-scatter.40
  639.5 30.1 reduce-scatter.28
  687.9 42.9 reduce-scatter.42
where the time goes:
time: 740 us; the launch traced here: 739 us
  waiting for transfers between devices  431 us (58%)
  blocking collectives  201 us (27%)
  starting transfers between devices  34.8 us (5%)
  matrix products  25.6 us (3%)
  local copies, waits for them, and re-layouts  19 us (3%)
  between operations  14.2 us (2%)
  other arithmetic  13.7 us (2%)
    reduce_scatter x4, waiting for transfers between devices, reverse_apply(): lax.psum_scatter(lax.dot_general(matrix, gathered, (((0,), (0,)), ((), ()...  168 us
    all_gather x5, blocking collectives, forward_apply(): gathered = lax.all_gather(vector, 'row', axis=0, tiled=True)  144 us
    unnamed x14, waiting for transfers between devices  104 us
    reduce_scatter x3, waiting for transfers between devices, forward_apply(): lax.psum_scatter(jnp.dot(matrix, gathered, preferred_element_type=jnp.flo...  96.2 us
    all_gather x4, blocking collectives, reverse_apply(): gathered = lax.all_gather(vector, 'col', axis=0, tiled=True)  56.7 us
    ppermute x10, waiting for transfers between devices, from_partner(): return lax.ppermute(block, axis, route)  36.8 us
    ppermute x10, starting transfers between devices, from_partner(): return lax.ppermute(block, axis, route)  34.3 us
    all_gather x1, waiting for transfers between devices, reverse_apply(): gathered = lax.all_gather(vector, 'col', axis=0, tiled=True)  25.4 us
  transfers between devices with their start and end apart: 21, of which 21 were waited for; matrix products, arithmetic and copies ran while one was open for 1% of the time, Pallas kernels for 0%

commit v1 on v0

--- a/solution.py
+++ b/solution.py
@@ -20,13 +20,23 @@
     return from_partner(block_data.astype(jnp.bfloat16), "leaf", leaf_bit).astype(block_data.dtype)
 
 
+def scatter_sum(block, axis, send_dtype):
+    count = lax.axis_size(axis)
+    pieces = block.astype(send_dtype).reshape(count, -1, block.shape[-1])
+    pieces = lax.all_to_all(pieces, axis, 0, 0, tiled=True)
+    return pieces.astype(jnp.float32).sum(0)
+
+
+def gather_rows(block, axis):
+    count = lax.axis_size(axis)
+    copies = jnp.broadcast_to(block[None], (count,) + block.shape)
+    return lax.all_to_all(copies, axis, 0, 0, tiled=True).reshape(-1, block.shape[-1])
+
+
 def forward_apply(matrix, vector, leaf_bits):
-    gathered = lax.all_gather(vector, "row", axis=0, tiled=True)
-    result = lax.psum_scatter(
-        jnp.dot(matrix, gathered, preferred_element_type=jnp.float32),
-        "col",
-        scatter_dimension=0,
-        tiled=True,
+    gathered = gather_rows(vector, "row")
+    result = scatter_sum(
+        jnp.dot(matrix, gathered, preferred_element_type=jnp.float32), "col", jnp.float32
     )
     for leaf_bit in leaf_bits:
         result = result + partner(result, leaf_bit)
@@ -34,15 +44,14 @@
 
 
 def reverse_apply(matrix, vector):
-    gathered = lax.all_gather(vector, "col", axis=0, tiled=True)
-    return lax.psum_scatter(
+    gathered = gather_rows(vector, "col")
+    return scatter_sum(
         lax.dot_general(
             matrix, gathered, (((0,), (0,)), ((), ())), preferred_element_type=jnp.float32
-        ).astype(jnp.bfloat16),
+        ),
         "row",
-        scatter_dimension=0,
-        tiled=True,
-    ).astype(jnp.float32)
+        jnp.bfloat16,
+    )
 
 
 def parent_slot(parent_rows, pivot_local, update_local):

time: 740 us -> 434 us (0.59)
  waiting for transfers between devices: 431 us -> 84.8 us
  blocking collectives: 201 us -> 249 us
  between operations: 14.2 us -> 1.24 us
  starting transfers between devices: 34.8 us -> 46.3 us
    reduce_scatter x7 -> x0, waiting for transfers between devices: 264 us -> none  [the longest x4 168 us: reverse_apply(): lax.psum_scatter(lax.dot_general(matrix, gathered, (((0,), (0,)), ((), ()...]
    all_to_all x0 -> x15, blocking collectives: none -> 249 us  [the longest x6 133 us: scatter_sum(): pieces = lax.all_to_all(pieces, axis, 0, 0, tiled=True)]
    all_gather x9 -> x0, blocking collectives: 201 us -> none  [the longest x5 144 us: forward_apply(): gathered = lax.all_gather(vector, 'row', axis=0, tiled=True)]
    unnamed x14 -> x0, waiting for transfers between devices: 104 us -> none
    all_to_all x0 -> x5, waiting for transfers between devices: none -> 42.7 us  [the longest x4 31 us: scatter_sum(): pieces = lax.all_to_all(pieces, axis, 0, 0, tiled=True)]
    all_gather x1 -> x0, waiting for transfers between devices: 25.4 us -> none  [reverse_apply(): gathered = lax.all_gather(vector, 'col', axis=0, tiled=True)]
    all_to_all x0 -> x5, starting transfers between devices: none -> 18.7 us  [the longest x4 13.9 us: scatter_sum(): pieces = lax.all_to_all(pieces, axis, 0, 0, tiled=True)]
    unnamed x27, local copies, waits for them, and re-layouts: 14.6 us -> 2.09 us
  transfers between devices with their start and end apart: 21 -> 15, of which waited for: 21 -> 15; matrix products, arithmetic and copies ran while one was open for 1% -> 1% of each run, Pallas kernels for 0% -> 0%
where the time goes in v1:
time: 434 us; the launch traced here: 433 us
  blocking collectives  249 us (57%)
  waiting for transfers between devices  84.8 us (20%)
  starting transfers between devices  46.3 us (11%)
  matrix products  21.1 us (5%)
  local copies, waits for them, and re-layouts  18.8 us (4%)
  other arithmetic  11.3 us (3%)
    all_to_all x6, blocking collectives, scatter_sum(): pieces = lax.all_to_all(pieces, axis, 0, 0, tiled=True)  133 us
    all_to_all x9, blocking collectives, gather_rows(): lax.all_to_all(copies, axis, 0, 0, tiled=True).reshape(-1, block.shape[-1])  116 us
    ppermute x10, waiting for transfers between devices, from_partner(): return lax.ppermute(block, axis, route)  42.1 us
    all_to_all x4, waiting for transfers between devices, scatter_sum(): pieces = lax.all_to_all(pieces, axis, 0, 0, tiled=True)  31 us
    ppermute x10, starting transfers between devices, from_partner(): return lax.ppermute(block, axis, route)  27.6 us
    all_to_all x4, starting transfers between devices, scatter_sum(): pieces = lax.all_to_all(pieces, axis, 0, 0, tiled=True)  13.9 us
    dot_general x5, matrix products, forward_apply(): jnp.dot(matrix, gathered, preferred_element_type=jnp.float32)  12.2 us
    all_to_all x1, waiting for transfers between devices, gather_rows(): lax.all_to_all(copies, axis, 0, 0, tiled=True).reshape(-1, block.shape[-1])  11.7 us
  transfers between devices with their start and end apart: 15, of which 15 were waited for; matrix products, arithmetic and copies ran while one was open for 1% of the time, Pallas kernels for 0%

profile of v1, /device:TPU:2, one launch (start us, length us, event | category | flops | bytes accessed | tf_op | source)
XLA Modules:
  0.0 432.6 jit_solution(3009701887003017294)
XLA Ops:
  0.6 1.1 convert_bitcast_fusion
  1.7 15.7 %all_to_all.100 = bf16[8,128,256]{2,1,0:T(8,128)(2,1)S(1)} all-to-all(bf16[8,128,256]{2,1,0:T(8,128)(2,1)S(1)} %broadcast_in_dim.42), channel_id=1, replica_groups=mesh['leaf'=4,'row'=8,'col'=8] {'row'}, dimensions={0} | all-to-all | bytes 1048576 | tf_op jit(solution)/shard_map/all_to_all | solution.py:33
  17.4 2.3 fusion.46
  19.8 19.2 %all_to_all.101 = f32[8,128,256]{2,1,0:T(8,128)S(1)} all-to-all(f32[8,128,256]{2,1,0:T(8,128)S(1)} %fusion.46), channel_id=1, replica_groups=mesh['leaf'=4,'row'=8,'col'=8] {'col'}, dimensions={0} | all-to-all | bytes 2097152 | tf_op jit(solution)/shard_map/all_to_all | solution.py:26
  39.1 12.7 %all_to_all.102 = bf16[8,128,256]{2,1,0:T(8,128)(2,1)S(1)} all-to-all(bf16[8,128,256]{2,1,0:T(8,128)(2,1)S(1)} %broadcast_in_dim.43), channel_id=1, replica_groups=mesh['leaf'=4,'row'=8,'col'=8] {'col'}, dimensions={0} | all-to-all | bytes 1048576 | tf_op jit(solution)/shard_map/all_to_all | solution.py:33
  51.8 2.3 fusion.18
  55.1 3.5 all-to-all-start.3
  58.6 9.4 %all-to-all-done.3 = bf16[8,128,256]{1,2,0:T(8,128)(2,1)S(1)} async-done(((bf16[8,128,256]{1,2,0:T(8,128)(2,1)}), bf16[8,128,256]{1,2,0:T(8,128)(2,1)S(1)}, u32[]{:S(2)}, u32[]{:S(2)}) %all-to-all-start.3) | async-done | bytes 524320 | tf_op jit(solution)/shard_map/all_to_all | solution.py:26
  68.2 3.4 collective-permute-start
  71.6 1.0 scatter_custom_fusion
  73.5 1.0 scatter_custom_fusion.1
  74.5 11.1 %all_to_all.103 = bf16[8,96,256]{2,1,0:T(8,128)(2,1)S(1)} all-to-all(bf16[8,96,256]{2,1,0:T(8,128)(2,1)S(1)} %broadcast_in_dim.44), channel_id=1, replica_groups=mesh['leaf'=4,'row'=8,'col'=8] {'row'}, dimensions={0} | all-to-all | bytes 786432 | tf_op jit(solution)/shard_map/all_to_all | solution.py:33
  85.6 2.0 convolution_bitcast_fusion.1
  87.6 3.0 copy.58
  90.6 26.0 %all_to_all.104 = f32[8,192,256]{2,1,0:T(8,128)} all-to-all(f32[8,192,256]{2,1,0:T(8,128)} %bitcast.145), channel_id=1, replica_groups=mesh['leaf'=4,'row'=8,'col'=8] {'col'}, dimensions={0} | all-to-all | bytes 3145728 | tf_op jit(solution)/shard_map/all_to_all | solution.py:26
  116.7 1.5 reduce_sum.92
  118.2 3.3 collective-permute-start.1
  121.5 4.5 %collective-permute-done.1 = bf16[192,256]{1,0:T(8,128)(2,1)S(1)} collective-permute-done((bf16[192,256]{1,0:T(8,128)(2,1)S(1)}, bf16[192,256]{1,0:T(8,128)(2,1)S(1)}, u32[]{:S(2)}, u32[]{:S(2)}) %collective-permute-start.1) | collective-permute-done | bytes 98336 | tf_op jit(solution)/shard_map/ppermute | solution.py:16
  126.7 0.9 broadcast_in_dim.49
  127.6 4.8 %all-to-all-start.6 = ((bf16[8,192,256]{2,1,0:T(8,128)(2,1)}), bf16[8,192,256]{2,1,0:T(8,128)(2,1)S(1)}, u32[]{:S(2)}, u32[]{:S(2)}) async-start(bf16[8,192,256]{2,1,0:T(8,128)(2,1)} %broadcast_in_dim.49), calls=%async_computation.6 | async-start | bytes 1572864 | tf_op jit(solution)/shard_map/all_to_all | solution.py:33
  132.4 11.7 %all-to-all-done.6 = bf16[8,192,256]{2,1,0:T(8,128)(2,1)S(1)} async-done(((bf16[8,192,256]{2,1,0:T(8,128)(2,1)}), bf16[8,192,256]{2,1,0:T(8,128)(2,1)S(1)}, u32[]{:S(2)}, u32[]{:S(2)}) %all-to-all-start.6) | async-done | bytes 786464 | tf_op jit(solution)/shard_map/all_to_all | solution.py:33
  144.1 2.7 fusion.22
  146.8 1.8 copy.59
  148.6 3.4 all-to-all-start.7
  152.8 6.4 %all-to-all-done.7 = bf16[8,64,256]{2,1,0:T(8,128)(2,1)S(1)} async-done(((bf16[8,64,256]{2,1,0:T(8,128)(2,1)}), bf16[8,64,256]{2,1,0:T(8,128)(2,1)S(1)}, u32[]{:S(2)}, u32[]{:S(2)}) %all-to-all-start.7) | async-done | bytes 262176 | tf_op jit(solution)/shard_map/all_to_all | solution.py:26
  160.1 2.1 collective-permute-start.2
  162.2 2.8 collective-permute-done.2
  165.0 5.4 %collective-permute-start.3 = (bf16[2,16,256]{2,1,0:T(8,128)(2,1)S(1)}, bf16[2,16,256]{2,1,0:T(8,128)(2,1)S(1)}, u32[]{:S(2)}, u32[]{:S(2)}) collective-permute-start(bf16[2,16,256]{2,1,0:T(8,128)(2,1)S(1)} %pad_maximum_fusion.4), channel_id=1, source_target_pairs={{0,128},{128,0},{64,192},{192,64},{1,129},{129,1},{65,193},{193,65... | collective-permute-start | bytes 49160 | tf_op jit(solution)/shard_map/ppermute | solution.py:16
  170.4 2.3 collective-permute-done.3
  172.7 1.0 scatter_fusion
  173.8 9.6 %all_to_all.105 = bf16[8,64,256]{2,1,0:T(8,128)(2,1)S(1)} all-to-all(bf16[8,64,256]{2,1,0:T(8,128)(2,1)S(1)} %broadcast_in_dim.50), channel_id=1, replica_groups=mesh['leaf'=4,'row'=8,'col'=8] {'row'}, dimensions={0} | all-to-all | bytes 524288 | tf_op jit(solution)/shard_map/all_to_all | solution.py:33
  183.4 2.3 fusion.47
  186.0 30.6 %all_to_all.106 = f32[8,256,256]{1,2,0:T(8,128)} all-to-all(f32[8,256,256]{1,2,0:T(8,128)S(1)} %bitcast.143), channel_id=1, replica_groups=mesh['leaf'=4,'row'=8,'col'=8] {'col'}, dimensions={0} | all-to-all | bytes 4194304 | tf_op jit(solution)/shard_map/all_to_all | solution.py:26
  216.6 1.8 reduce_sum.94
  218.4 2.1 collective-permute-start.4
  220.5 6.6 %collective-permute-done.4 = bf16[256,256]{0,1:T(8,128)(2,1)S(1)} collective-permute-done((bf16[256,256]{0,1:T(8,128)(2,1)S(1)}, bf16[256,256]{0,1:T(8,128)(2,1)S(1)}, u32[]{:S(2)}, u32[]{:S(2)}) %collective-permute-start.4) | collective-permute-done | bytes 131104 | tf_op jit(solution)/shard_map/ppermute | solution.py:16
  227.0 5.4 %collective-permute-start.5 = (bf16[256,256]{0,1:T(8,128)(2,1)S(1)}, bf16[256,256]{0,1:T(8,128)(2,1)S(1)}, u32[]{:S(2)}, u32[]{:S(2)}) collective-permute-start(bf16[256,256]{0,1:T(8,128)(2,1)S(1)} %fusion.24), channel_id=1, source_target_pairs={{0,128},{128,0},{64,192},{192,64},{1,129},{129,1},{65,193},{193,65... | collective-permute-start | bytes 393224 | tf_op jit(solution)/shard_map/ppermute | solution.py:16
  232.5 6.8 %collective-permute-done.5 = bf16[256,256]{0,1:T(8,128)(2,1)S(1)} collective-permute-done((bf16[256,256]{0,1:T(8,128)(2,1)S(1)}, bf16[256,256]{0,1:T(8,128)(2,1)S(1)}, u32[]{:S(2)}, u32[]{:S(2)}) %collective-permute-start.5) | collective-permute-done | bytes 131104 | tf_op jit(solution)/shard_map/ppermute | solution.py:16
  239.5 18.4 %all_to_all.107 = bf16[8,256,256]{2,1,0:T(8,128)(2,1)S(1)} all-to-all(bf16[8,256,256]{2,1,0:T(8,128)(2,1)S(1)} %broadcast_in_dim.51), channel_id=1, replica_groups=mesh['leaf'=4,'row'=8,'col'=8] {'col'}, dimensions={0} | all-to-all | bytes 2097152 | tf_op jit(solution)/shard_map/all_to_all | solution.py:33
  259.4 3.6 all-to-all-start.11
  263.0 7.0 %all-to-all-done.11 = bf16[8,64,256]{2,1,0:T(8,128)(2,1)S(1)} async-done(((bf16[8,64,256]{2,1,0:T(8,128)(2,1)}), bf16[8,64,256]{2,1,0:T(8,128)(2,1)S(1)}, u32[]{:S(2)}, u32[]{:S(2)}) %all-to-all-start.11) | async-done | bytes 262176 | tf_op jit(solution)/shard_map/all_to_all | solution.py:26
  270.7 2.6 collective-permute-start.6
  273.3 5.1 %collective-permute-done.6 = bf16[2,16,256]{2,1,0:T(8,128)(2,1)S(1)} collective-permute-done((bf16[2,16,256]{2,1,0:T(8,128)(2,1)S(1)}, bf16[2,16,256]{2,1,0:T(8,128)(2,1)S(1)}, u32[]{:S(2)}, u32[]{:S(2)}) %collective-permute-start.6) | collective-permute-done | bytes 16416 | tf_op jit(solution)/shard_map/ppermute | solution.py:16
  278.4 1.3 collective-permute-start.7
  279.9 3.3 collective-permute-done.7
  283.9 9.6 %all_to_all.108 = bf16[8,64,256]{2,1,0:T(8,128)(2,1)S(1)} all-to-all(bf16[8,64,256]{2,1,0:T(8,128)(2,1)S(1)} %broadcast_in_dim.53), channel_id=1, replica_groups=mesh['leaf'=4,'row'=8,'col'=8] {'row'}, dimensions={0} | all-to-all | bytes 524288 | tf_op jit(solution)/shard_map/all_to_all | solution.py:33
  293.6 3.2 convolution_bitcast_fusion
  296.8 3.0 copy.64
  299.8 26.1 %all_to_all.109 = f32[8,192,256]{2,1,0:T(8,128)} all-to-all(f32[8,192,256]{2,1,0:T(8,128)} %bitcast.146), channel_id=1, replica_groups=mesh['leaf'=4,'row'=8,'col'=8] {'col'}, dimensions={0} | all-to-all | bytes 3145728 | tf_op jit(solution)/shard_map/all_to_all | solution.py:26
  325.9 1.5 reduce_sum.96
  327.4 1.4 collective-permute-start.8
  328.9 5.8 %collective-permute-done.8 = bf16[192,256]{1,0:T(8,128)(2,1)S(1)} collective-permute-done((bf16[192,256]{1,0:T(8,128)(2,1)S(1)}, bf16[192,256]{1,0:T(8,128)(2,1)S(1)}, u32[]{:S(2)}, u32[]{:S(2)}) %collective-permute-start.8) | collective-permute-done | bytes 98336 | tf_op jit(solution)/shard_map/ppermute | solution.py:16
  334.8 15.5 %all_to_all.110 = bf16[8,192,256]{2,1,0:T(8,128)(2,1)S(1)} all-to-all(bf16[8,192,256]{2,1,0:T(8,128)(2,1)S(1)} %broadcast_in_dim.54), channel_id=1, replica_groups=mesh['leaf'=4,'row'=8,'col'=8] {'col'}, dimensions={0} | all-to-all | bytes 1572864 | tf_op jit(solution)/shard_map/all_to_all | solution.py:33
  351.1 0.9 copy.65
  352.0 3.5 all-to-all-start.15
  355.5 8.3 %all-to-all-done.15 = bf16[8,96,256]{2,1,0:T(8,128)(2,1)S(1)} async-done(((bf16[8,96,256]{2,1,0:T(8,128)(2,1)}), bf16[8,96,256]{2,1,0:T(8,128)(2,1)S(1)}, u32[]{:S(2)}, u32[]{:S(2)}) %all-to-all-start.15) | async-done | bytes 393248 | tf_op jit(solution)/shard_map/all_to_all | solution.py:26
  366.4 4.0 collective-permute-done.9
  370.5 11.1 %all_to_all.111 = bf16[8,128,256]{2,1,0:T(8,128)(2,1)S(1)} all-to-all(bf16[8,128,256]{2,1,0:T(8,128)(2,1)S(1)} %broadcast_in_dim.55), channel_id=1, replica_groups=mesh['leaf'=4,'row'=8,'col'=8] {'row'}, dimensions={0} | all-to-all | bytes 1048576 | tf_op jit(solution)/shard_map/all_to_all | solution.py:33
  381.6 2.3 fusion.6
  384.0 18.6 %all_to_all.112 = f32[8,128,256]{1,2,0:T(8,128)S(1)} all-to-all(f32[8,128,256]{1,2,0:T(8,128)S(1)} %bitcast.147), channel_id=1, replica_groups=mesh['leaf'=4,'row'=8,'col'=8] {'col'}, dimensions={0} | all-to-all | bytes 2097152 | tf_op jit(solution)/shard_map/all_to_all | solution.py:26
  403.3 1.0 copy.68
  404.4 12.7 %all_to_all.113 = bf16[8,128,256]{2,1,0:T(8,128)(2,1)S(1)} all-to-all(bf16[8,128,256]{2,1,0:T(8,128)(2,1)S(1)} %broadcast_in_dim.56), channel_id=1, replica_groups=mesh['leaf'=4,'row'=8,'col'=8] {'col'}, dimensions={0} | all-to-all | bytes 1048576 | tf_op jit(solution)/shard_map/all_to_all | solution.py:33
  417.0 2.3 fusion.15
  419.5 12.4 %all_to_all.114 = bf16[8,128,256]{1,2,0:T(8,128)(2,1)S(1)} all-to-all(bf16[8,128,256]{1,2,0:T(8,128)(2,1)S(1)} %bitcast.151), channel_id=1, replica_groups=mesh['leaf'=4,'row'=8,'col'=8] {'row'}, dimensions={0} | all-to-all | bytes 1048576 | tf_op jit(solution)/shard_map/all_to_all | solution.py:26
  (103 shorter events, 13.4 us)
Async XLA Ops:
  0.6 85.0 %copy-start = (bf16[1536,768]{1,0:T(8,128)(2,1)S(1)}, bf16[1536,768]{1,0:T(8,128)(2,1)}, u32[]{:S(2)}) copy-start(bf16[1536,768]{1,0:T(8,128)(2,1)} %param.15) | copy-start | bytes 7077892
  39.0 15.1 %copy-start.4 = (f32[128,256]{1,0:T(8,128)}, f32[128,256]{1,0:T(8,128)S(1)}, u32[]{:S(2)}) copy-start(f32[128,256]{1,0:T(8,128)S(1)} %reduce_sum.90) | copy-start | bytes 393220
  51.8 6.8 %copy-start.12 = (s32[1,1,1,2,64]{4,3,2,1,0:T(2,128)S(1)}, s32[1,1,1,2,64]{4,3,2,1,0:T(2,128)}, u32[]{:S(2)}) copy-start(s32[1,1,1,2,64]{4,3,2,1,0:T(2,128)} %param.18) | copy-start | bytes 1540
  54.2 17.4 %copy-start.10 = (f32[1,1,1,96,256]{4,3,2,1,0:T(8,128)S(1)}, f32[1,1,1,96,256]{4,3,2,1,0:T(8,128)}, u32[]{:S(2)}) copy-start(f32[1,1,1,96,256]{4,3,2,1,0:T(8,128)} %param.11) | copy-start | bytes 294916
  55.1 12.9 %all-to-all-start.3 = ((bf16[8,128,256]{1,2,0:T(8,128)(2,1)}), bf16[8,128,256]{1,2,0:T(8,128)(2,1)S(1)}, u32[]{:S(2)}, u32[]{:S(2)}) async-start(bf16[8,128,256]{1,2,0:T(8,128)(2,1)} %bitcast.140), calls=%async_computation.3 | async-start | bytes 1048576 | tf_op jit(solution)/shard_map/all_to_all | solution.py:26
  68.2 5.3 %collective-permute-start = (bf16[64,256]{1,0:T(8,128)(2,1)S(1)}, bf16[64,256]{1,0:T(8,128)(2,1)S(1)}, u32[]{:S(2)}, u32[]{:S(2)}) collective-permute-start(bf16[64,256]{1,0:T(8,128)(2,1)S(1)} %fusion.34), channel_id=1, source_target_pairs={{0,64},{64,0},{128,192},{192,128},{1,65},{65,1},{129,193},{193,129... | collective-permute-start | bytes 98312 | tf_op jit(solution)/shard_map/ppermute | solution.py:16
  74.5 13.1 %copy-start.6 = (f32[160,256]{1,0:T(8,128)}, f32[160,256]{1,0:T(8,128)S(1)}, u32[]{:S(2)}) copy-start(f32[160,256]{1,0:T(8,128)S(1)} %scatter_custom_fusion.1) | copy-start | bytes 491524
  116.7 15.7 %copy-start.11 = (s32[1,1,1,4,16]{4,3,2,1,0:T(4,128)S(1)}, s32[1,1,1,4,16]{4,3,2,1,0:T(4,128)}, u32[]{:S(2)}) copy-start(s32[1,1,1,4,16]{4,3,2,1,0:T(4,128)} %param.19) | copy-start | bytes 772
  118.2 7.8 %collective-permute-start.1 = (bf16[192,256]{1,0:T(8,128)(2,1)S(1)}, bf16[192,256]{1,0:T(8,128)(2,1)S(1)}, u32[]{:S(2)}, u32[]{:S(2)}) collective-permute-start(bf16[192,256]{1,0:T(8,128)(2,1)S(1)} %convert_element_type.156), channel_id=1, source_target_pairs={{0,64},{64,0},{128,192},{192,128},{1,65},{65,1},{129,193},{193,129... | collective-permute-start | bytes 294920 | tf_op jit(solution)/shard_map/ppermute | solution.py:16
  126.0 0.6 copy-start.7
  127.6 16.5 %all-to-all-start.6 = ((bf16[8,192,256]{2,1,0:T(8,128)(2,1)}), bf16[8,192,256]{2,1,0:T(8,128)(2,1)S(1)}, u32[]{:S(2)}, u32[]{:S(2)}) async-start(bf16[8,192,256]{2,1,0:T(8,128)(2,1)} %broadcast_in_dim.49), calls=%async_computation.6 | async-start | bytes 1572864 | tf_op jit(solution)/shard_map/all_to_all | solution.py:33
  144.1 28.7 %copy-start.1 = (f32[1,1,1,64,256]{4,3,2,1,0:T(8,128)S(1)}, f32[1,1,1,64,256]{4,3,2,1,0:T(8,128)}, u32[]{:S(2)}) copy-start(f32[1,1,1,64,256]{4,3,2,1,0:T(8,128)} %param.12) | copy-start | bytes 196612
  148.6 10.6 %all-to-all-start.7 = ((bf16[8,64,256]{2,1,0:T(8,128)(2,1)}), bf16[8,64,256]{2,1,0:T(8,128)(2,1)S(1)}, u32[]{:S(2)}, u32[]{:S(2)}) async-start(bf16[8,64,256]{2,1,0:T(8,128)(2,1)} %bitcast.27), calls=%async_computation.7 | async-start | bytes 524288 | tf_op jit(solution)/shard_map/all_to_all | solution.py:26
  160.1 4.9 %collective-permute-start.2 = (bf16[2,16,256]{2,1,0:T(8,128)(2,1)S(1)}, bf16[2,16,256]{2,1,0:T(8,128)(2,1)S(1)}, u32[]{:S(2)}, u32[]{:S(2)}) collective-permute-start(bf16[2,16,256]{2,1,0:T(8,128)(2,1)S(1)} %pad_maximum_fusion.3), channel_id=1, source_target_pairs={{0,64},{64,0},{128,192},{192,128},{1,65},{65,1},{129,193},{193,129... | collective-permute-start | bytes 49160 | tf_op jit(solution)/shard_map/ppermute | solution.py:16
  165.0 7.7 %collective-permute-start.3 = (bf16[2,16,256]{2,1,0:T(8,128)(2,1)S(1)}, bf16[2,16,256]{2,1,0:T(8,128)(2,1)S(1)}, u32[]{:S(2)}, u32[]{:S(2)}) collective-permute-start(bf16[2,16,256]{2,1,0:T(8,128)(2,1)S(1)} %pad_maximum_fusion.4), channel_id=1, source_target_pairs={{0,128},{128,0},{64,192},{192,64},{1,129},{129,1},{65,193},{193,65... | collective-permute-start | bytes 49160 | tf_op jit(solution)/shard_map/ppermute | solution.py:16
  218.4 8.7 %collective-permute-start.4 = (bf16[256,256]{0,1:T(8,128)(2,1)S(1)}, bf16[256,256]{0,1:T(8,128)(2,1)S(1)}, u32[]{:S(2)}, u32[]{:S(2)}) collective-permute-start(bf16[256,256]{0,1:T(8,128)(2,1)S(1)} %convert_element_type.164), channel_id=1, source_target_pairs={{0,64},{64,0},{128,192},{192,128},{1,65},{65,1},{129,193},{193,129... | collective-permute-start | bytes 393224 | tf_op jit(solution)/shard_map/ppermute | solution.py:16
  227.0 12.2 %collective-permute-start.5 = (bf16[256,256]{0,1:T(8,128)(2,1)S(1)}, bf16[256,256]{0,1:T(8,128)(2,1)S(1)}, u32[]{:S(2)}, u32[]{:S(2)}) collective-permute-start(bf16[256,256]{0,1:T(8,128)(2,1)S(1)} %fusion.24), channel_id=1, source_target_pairs={{0,128},{128,0},{64,192},{192,64},{1,129},{129,1},{65,193},{193,65... | collective-permute-start | bytes 393224 | tf_op jit(solution)/shard_map/ppermute | solution.py:16
  239.4 18.5 %copy-start.2 = (bf16[2048,512]{1,0:T(8,128)(2,1)S(1)}, bf16[2048,512]{1,0:T(8,128)(2,1)}, u32[]{:S(2)}) copy-start(bf16[2048,512]{1,0:T(8,128)(2,1)} %param.17) | copy-start | bytes 6291460
  259.4 10.6 %all-to-all-start.11 = ((bf16[8,64,256]{2,1,0:T(8,128)(2,1)}), bf16[8,64,256]{2,1,0:T(8,128)(2,1)S(1)}, u32[]{:S(2)}, u32[]{:S(2)}) async-start(bf16[8,64,256]{2,1,0:T(8,128)(2,1)} %bitcast.34), calls=%async_computation.11 | async-start | bytes 524288 | tf_op jit(solution)/shard_map/all_to_all | solution.py:26
  270.0 26.8 %copy-start.3 = (f32[64,256]{1,0:T(8,128)}, f32[64,256]{1,0:T(8,128)S(1)}, u32[]{:S(2)}) copy-start(f32[64,256]{1,0:T(8,128)S(1)} %convert_reduce_fusion.3) | copy-start | bytes 196612
  270.7 7.7 %collective-permute-start.6 = (bf16[2,16,256]{2,1,0:T(8,128)(2,1)S(1)}, bf16[2,16,256]{2,1,0:T(8,128)(2,1)S(1)}, u32[]{:S(2)}, u32[]{:S(2)}) collective-permute-start(bf16[2,16,256]{2,1,0:T(8,128)(2,1)S(1)} %pad_maximum_fusion.5), channel_id=1, source_target_pairs={{0,128},{128,0},{64,192},{192,64},{1,129},{129,1},{65,193},{193,65... | collective-permute-start | bytes 49160 | tf_op jit(solution)/shard_map/ppermute | solution.py:16
  278.4 4.8 %collective-permute-start.7 = (bf16[2,16,256]{2,1,0:T(8,128)(2,1)S(1)}, bf16[2,16,256]{2,1,0:T(8,128)(2,1)S(1)}, u32[]{:S(2)}, u32[]{:S(2)}) collective-permute-start(bf16[2,16,256]{2,1,0:T(8,128)(2,1)S(1)} %pad_maximum_fusion.6), channel_id=1, source_target_pairs={{0,64},{64,0},{128,192},{192,128},{1,65},{65,1},{129,193},{193,129... | collective-permute-start | bytes 49160 | tf_op jit(solution)/shard_map/ppermute | solution.py:16
  299.8 34.9 %copy-start.8 = (bf16[192,256]{1,0:T(8,128)(2,1)S(1)}, bf16[192,256]{1,0:T(8,128)(2,1)}, u32[]{:S(2)}) copy-start(bf16[192,256]{1,0:T(8,128)(2,1)} %copy-done.7) | copy-start | bytes 294916
  327.4 7.3 %collective-permute-start.8 = (bf16[192,256]{1,0:T(8,128)(2,1)S(1)}, bf16[192,256]{1,0:T(8,128)(2,1)S(1)}, u32[]{:S(2)}, u32[]{:S(2)}) collective-permute-start(bf16[192,256]{1,0:T(8,128)(2,1)S(1)} %convert_element_type.174), channel_id=1, source_target_pairs={{0,64},{64,0},{128,192},{192,128},{1,65},{65,1},{129,193},{193,129... | collective-permute-start | bytes 294920 | tf_op jit(solution)/shard_map/ppermute | solution.py:16
  352.0 11.7 %all-to-all-start.15 = ((bf16[8,96,256]{2,1,0:T(8,128)(2,1)}), bf16[8,96,256]{2,1,0:T(8,128)(2,1)S(1)}, u32[]{:S(2)}, u32[]{:S(2)}) async-start(bf16[8,96,256]{2,1,0:T(8,128)(2,1)} %bitcast.45), calls=%async_computation.15 | async-start | bytes 786432 | tf_op jit(solution)/shard_map/all_to_all | solution.py:26
  363.8 0.6 copy-start.9
  365.2 5.3 %collective-permute-start.9 = (bf16[64,256]{1,0:T(8,128)(2,1)S(1)}, bf16[64,256]{1,0:T(8,128)(2,1)S(1)}, u32[]{:S(2)}, u32[]{:S(2)}) collective-permute-start(bf16[64,256]{1,0:T(8,128)(2,1)S(1)} %gather_fusion.4), channel_id=1, source_target_pairs={{0,64},{64,0},{128,192},{192,128},{1,65},{65,1},{129,193},{193,129... | collective-permute-start | bytes 98312 | tf_op jit(solution)/shard_map/ppermute | solution.py:16
  384.0 20.3 %copy-start.5 = (f32[128,256]{1,0:T(8,128)S(1)}, f32[128,256]{1,0:T(8,128)}, u32[]{:S(2)}) copy-start(f32[128,256]{1,0:T(8,128)} %copy-done.4) | copy-start | bytes 393220

commit v2 on v1

--- a/solution.py
+++ b/solution.py
@@ -36,7 +36,7 @@
 def forward_apply(matrix, vector, leaf_bits):
     gathered = gather_rows(vector, "row")
     result = scatter_sum(
-        jnp.dot(matrix, gathered, preferred_element_type=jnp.float32), "col", jnp.float32
+        jnp.dot(matrix, gathered, preferred_element_type=jnp.float32), "col", jnp.bfloat16
     )
     for leaf_bit in leaf_bits:
         result = result + partner(result, leaf_bit)

time: 434 us -> 380 us (0.88)
  blocking collectives: 249 us -> 205 us
  other arithmetic: 11.3 us -> 6.22 us
    all_to_all x6, blocking collectives: 133 us -> 88.5 us  [scatter_sum(): pieces = lax.all_to_all(pieces, axis, 0, 0, tiled=True)]
    dot_general x2 -> x0, local copies, waits for them, and re-layouts: 6.07 us -> none  [forward_apply(): jnp.dot(matrix, gathered, preferred_element_type=jnp.float32)]
    reduce_sum x10, other arithmetic: 5.85 us -> 0.75 us  [scatter_sum(): return pieces.astype(jnp.float32).sum(0)]
where the time goes in v2:
time: 380 us; the launch traced here: 379 us
  blocking collectives  205 us (54%)
  waiting for transfers between devices  84.9 us (22%)
  starting transfers between devices  46.4 us (12%)
  matrix products  19.7 us (5%)
  local copies, waits for them, and re-layouts  14.9 us (4%)
  other arithmetic  6.22 us (2%)
    all_to_all x9, blocking collectives, gather_rows(): lax.all_to_all(copies, axis, 0, 0, tiled=True).reshape(-1, block.shape[-1])  117 us
    all_to_all x6, blocking collectives, scatter_sum(): pieces = lax.all_to_all(pieces, axis, 0, 0, tiled=True)  88.5 us
    ppermute x10, waiting for transfers between devices, from_partner(): return lax.ppermute(block, axis, route)  42 us
    all_to_all x4, waiting for transfers between devices, scatter_sum(): pieces = lax.all_to_all(pieces, axis, 0, 0, tiled=True)  31.2 us
    ppermute x10, starting transfers between devices, from_partner(): return lax.ppermute(block, axis, route)  27.8 us
    all_to_all x4, starting transfers between devices, scatter_sum(): pieces = lax.all_to_all(pieces, axis, 0, 0, tiled=True)  13.8 us
    all_to_all x1, waiting for transfers between devices, gather_rows(): lax.all_to_all(copies, axis, 0, 0, tiled=True).reshape(-1, block.shape[-1])  11.7 us
    dot_general x5, matrix products, forward_apply(): jnp.dot(matrix, gathered, preferred_element_type=jnp.float32)  11.6 us
  transfers between devices with their start and end apart: 15, of which 15 were waited for; matrix products, arithmetic and copies ran while one was open for 1% of the time, Pallas kernels for 0%

profile of v2, /device:TPU:2, one launch (start us, length us, event | category | flops | bytes accessed | tf_op | source)
XLA Modules:
  0.0 378.6 jit_solution(10220499604108640890)
XLA Ops:
  0.6 1.1 convert_bitcast_fusion
  1.7 15.7 %all_to_all.100 = bf16[8,128,256]{2,1,0:T(8,128)(2,1)S(1)} all-to-all(bf16[8,128,256]{2,1,0:T(8,128)(2,1)S(1)} %broadcast_in_dim.42), channel_id=1, replica_groups=mesh['leaf'=4,'row'=8,'col'=8] {'row'}, dimensions={0} | all-to-all | bytes 1048576 | tf_op jit(solution)/shard_map/all_to_all | solution.py:33
  17.4 2.3 fusion.10
  19.8 13.7 %all_to_all.101 = bf16[8,128,256]{2,1,0:T(8,128)(2,1)S(1)} all-to-all(bf16[8,128,256]{2,1,0:T(8,128)(2,1)S(1)} %bitcast.161), channel_id=1, replica_groups=mesh['leaf'=4,'row'=8,'col'=8] {'col'}, dimensions={0} | all-to-all | bytes 1048576 | tf_op jit(solution)/shard_map/all_to_all | solution.py:26
  33.5 12.8 %all_to_all.102 = bf16[8,128,256]{2,1,0:T(8,128)(2,1)S(1)} all-to-all(bf16[8,128,256]{2,1,0:T(8,128)(2,1)S(1)} %broadcast_in_dim.43), channel_id=1, replica_groups=mesh['leaf'=4,'row'=8,'col'=8] {'col'}, dimensions={0} | all-to-all | bytes 1048576 | tf_op jit(solution)/shard_map/all_to_all | solution.py:33
  47.1 0.9 copy.87
  47.9 3.5 all-to-all-start.3
  51.5 9.4 %all-to-all-done.3 = bf16[8,128,256]{1,2,0:T(8,128)(2,1)S(1)} async-done(((bf16[8,128,256]{1,2,0:T(8,128)(2,1)}), bf16[8,128,256]{1,2,0:T(8,128)(2,1)S(1)}, u32[]{:S(2)}, u32[]{:S(2)}) %all-to-all-start.3) | async-done | bytes 524320 | tf_op jit(solution)/shard_map/all_to_all | solution.py:26
  61.1 3.4 collective-permute-start
  64.5 1.0 scatter_custom_fusion
  65.5 0.8 collective-permute-done
  66.3 1.0 scatter_custom_fusion.1
  67.4 11.1 %all_to_all.103 = bf16[8,96,256]{2,1,0:T(8,128)(2,1)S(1)} all-to-all(bf16[8,96,256]{2,1,0:T(8,128)(2,1)S(1)} %broadcast_in_dim.44), channel_id=1, replica_groups=mesh['leaf'=4,'row'=8,'col'=8] {'row'}, dimensions={0} | all-to-all | bytes 786432 | tf_op jit(solution)/shard_map/all_to_all | solution.py:33
  78.5 1.7 fusion.1
  80.2 1.4 copy.58
  81.6 15.6 %all_to_all.104 = bf16[8,192,256]{2,1,0:T(8,128)(2,1)S(1)} all-to-all(bf16[8,192,256]{2,1,0:T(8,128)(2,1)S(1)} %bitcast.147), channel_id=1, replica_groups=mesh['leaf'=4,'row'=8,'col'=8] {'col'}, dimensions={0} | all-to-all | bytes 1572864 | tf_op jit(solution)/shard_map/all_to_all | solution.py:26
  97.3 3.3 collective-permute-start.1
  100.6 4.5 %collective-permute-done.1 = bf16[192,256]{1,0:T(8,128)(2,1)S(1)} collective-permute-done((bf16[192,256]{1,0:T(8,128)(2,1)S(1)}, bf16[192,256]{1,0:T(8,128)(2,1)S(1)}, u32[]{:S(2)}, u32[]{:S(2)}) %collective-permute-start.1) | collective-permute-done | bytes 98336 | tf_op jit(solution)/shard_map/ppermute | solution.py:16
  105.2 0.9 broadcast_in_dim.49
  106.1 4.9 %all-to-all-start.6 = ((bf16[8,192,256]{2,1,0:T(8,128)(2,1)}), bf16[8,192,256]{2,1,0:T(8,128)(2,1)S(1)}, u32[]{:S(2)}, u32[]{:S(2)}) async-start(bf16[8,192,256]{2,1,0:T(8,128)(2,1)} %broadcast_in_dim.49), calls=%async_computation.6 | async-start | bytes 1572864 | tf_op jit(solution)/shard_map/all_to_all | solution.py:33
  111.0 11.7 %all-to-all-done.6 = bf16[8,192,256]{2,1,0:T(8,128)(2,1)S(1)} async-done(((bf16[8,192,256]{2,1,0:T(8,128)(2,1)}), bf16[8,192,256]{2,1,0:T(8,128)(2,1)S(1)}, u32[]{:S(2)}, u32[]{:S(2)}) %all-to-all-start.6) | async-done | bytes 786464 | tf_op jit(solution)/shard_map/all_to_all | solution.py:33
  122.7 2.7 fusion.32
  125.4 1.8 copy.59
  127.2 3.4 all-to-all-start.7
  131.4 6.4 %all-to-all-done.7 = bf16[8,64,256]{2,1,0:T(8,128)(2,1)S(1)} async-done(((bf16[8,64,256]{2,1,0:T(8,128)(2,1)}), bf16[8,64,256]{2,1,0:T(8,128)(2,1)S(1)}, u32[]{:S(2)}, u32[]{:S(2)}) %all-to-all-start.7) | async-done | bytes 262176 | tf_op jit(solution)/shard_map/all_to_all | solution.py:26
  137.8 0.9 slice_subtract_fusion
  138.7 2.1 collective-permute-start.2
  140.8 2.8 collective-permute-done.2
  143.6 5.4 %collective-permute-start.3 = (bf16[2,16,256]{2,1,0:T(8,128)(2,1)S(1)}, bf16[2,16,256]{2,1,0:T(8,128)(2,1)S(1)}, u32[]{:S(2)}, u32[]{:S(2)}) collective-permute-start(bf16[2,16,256]{2,1,0:T(8,128)(2,1)S(1)} %pad_maximum_fusion.4), channel_id=1, source_target_pairs={{0,128},{128,0},{64,192},{192,64},{1,129},{129,1},{65,193},{193,65... | collective-permute-start | bytes 49160 | tf_op jit(solution)/shard_map/ppermute | solution.py:16
  149.0 2.3 collective-permute-done.3
  151.4 1.0 scatter_fusion
  152.4 9.6 %all_to_all.105 = bf16[8,64,256]{2,1,0:T(8,128)(2,1)S(1)} all-to-all(bf16[8,64,256]{2,1,0:T(8,128)(2,1)S(1)} %broadcast_in_dim.50), channel_id=1, replica_groups=mesh['leaf'=4,'row'=8,'col'=8] {'row'}, dimensions={0} | all-to-all | bytes 524288 | tf_op jit(solution)/shard_map/all_to_all | solution.py:33
  162.0 2.4 convolution_convert_fusion
  164.5 18.5 %all_to_all.106 = bf16[8,256,256]{1,2,0:T(8,128)(2,1)S(1)} all-to-all(bf16[8,256,256]{1,2,0:T(8,128)(2,1)S(1)} %bitcast.146), channel_id=1, replica_groups=mesh['leaf'=4,'row'=8,'col'=8] {'col'}, dimensions={0} | all-to-all | bytes 2097152 | tf_op jit(solution)/shard_map/all_to_all | solution.py:26
  183.1 2.1 collective-permute-start.4
  185.2 6.6 %collective-permute-done.4 = bf16[256,256]{0,1:T(8,128)(2,1)S(1)} collective-permute-done((bf16[256,256]{0,1:T(8,128)(2,1)S(1)}, bf16[256,256]{0,1:T(8,128)(2,1)S(1)}, u32[]{:S(2)}, u32[]{:S(2)}) %collective-permute-start.4) | collective-permute-done | bytes 131104 | tf_op jit(solution)/shard_map/ppermute | solution.py:16
  191.8 5.4 %collective-permute-start.5 = (bf16[256,256]{0,1:T(8,128)(2,1)S(1)}, bf16[256,256]{0,1:T(8,128)(2,1)S(1)}, u32[]{:S(2)}, u32[]{:S(2)}) collective-permute-start(bf16[256,256]{0,1:T(8,128)(2,1)S(1)} %fusion.34), channel_id=1, source_target_pairs={{0,128},{128,0},{64,192},{192,64},{1,129},{129,1},{65,193},{193,65... | collective-permute-start | bytes 393224 | tf_op jit(solution)/shard_map/ppermute | solution.py:16
  197.2 6.7 %collective-permute-done.5 = bf16[256,256]{0,1:T(8,128)(2,1)S(1)} collective-permute-done((bf16[256,256]{0,1:T(8,128)(2,1)S(1)}, bf16[256,256]{0,1:T(8,128)(2,1)S(1)}, u32[]{:S(2)}, u32[]{:S(2)}) %collective-permute-start.5) | collective-permute-done | bytes 131104 | tf_op jit(solution)/shard_map/ppermute | solution.py:16
  204.2 18.5 %all_to_all.107 = bf16[8,256,256]{2,1,0:T(8,128)(2,1)S(1)} all-to-all(bf16[8,256,256]{2,1,0:T(8,128)(2,1)S(1)} %broadcast_in_dim.51), channel_id=1, replica_groups=mesh['leaf'=4,'row'=8,'col'=8] {'col'}, dimensions={0} | all-to-all | bytes 2097152 | tf_op jit(solution)/shard_map/all_to_all | solution.py:33
  223.5 0.8 copy.63
  224.3 3.4 all-to-all-start.11
  227.7 7.1 %all-to-all-done.11 = bf16[8,64,256]{2,1,0:T(8,128)(2,1)S(1)} async-done(((bf16[8,64,256]{2,1,0:T(8,128)(2,1)}), bf16[8,64,256]{2,1,0:T(8,128)(2,1)S(1)}, u32[]{:S(2)}, u32[]{:S(2)}) %all-to-all-start.11) | async-done | bytes 262176 | tf_op jit(solution)/shard_map/all_to_all | solution.py:26
  235.6 2.8 collective-permute-start.6
  238.4 5.1 %collective-permute-done.6 = bf16[2,16,256]{2,1,0:T(8,128)(2,1)S(1)} collective-permute-done((bf16[2,16,256]{2,1,0:T(8,128)(2,1)S(1)}, bf16[2,16,256]{2,1,0:T(8,128)(2,1)S(1)}, u32[]{:S(2)}, u32[]{:S(2)}) %collective-permute-start.6) | collective-permute-done | bytes 16416 | tf_op jit(solution)/shard_map/ppermute | solution.py:16
  243.5 1.3 collective-permute-start.7
  245.0 3.3 collective-permute-done.7
  249.6 9.6 %all_to_all.108 = bf16[8,64,256]{2,1,0:T(8,128)(2,1)S(1)} all-to-all(bf16[8,64,256]{2,1,0:T(8,128)(2,1)S(1)} %broadcast_in_dim.53), channel_id=1, replica_groups=mesh['leaf'=4,'row'=8,'col'=8] {'row'}, dimensions={0} | all-to-all | bytes 524288 | tf_op jit(solution)/shard_map/all_to_all | solution.py:33
  259.3 2.9 fusion
  262.2 1.4 copy.64
  263.6 15.7 %all_to_all.109 = bf16[8,192,256]{2,1,0:T(8,128)(2,1)S(1)} all-to-all(bf16[8,192,256]{2,1,0:T(8,128)(2,1)S(1)} %bitcast.148), channel_id=1, replica_groups=mesh['leaf'=4,'row'=8,'col'=8] {'col'}, dimensions={0} | all-to-all | bytes 1572864 | tf_op jit(solution)/shard_map/all_to_all | solution.py:26
  279.4 1.4 collective-permute-start.8
  280.8 5.8 %collective-permute-done.8 = bf16[192,256]{1,0:T(8,128)(2,1)S(1)} collective-permute-done((bf16[192,256]{1,0:T(8,128)(2,1)S(1)}, bf16[192,256]{1,0:T(8,128)(2,1)S(1)}, u32[]{:S(2)}, u32[]{:S(2)}) %collective-permute-start.8) | collective-permute-done | bytes 98336 | tf_op jit(solution)/shard_map/ppermute | solution.py:16
  286.8 15.6 %all_to_all.110 = bf16[8,192,256]{2,1,0:T(8,128)(2,1)S(1)} all-to-all(bf16[8,192,256]{2,1,0:T(8,128)(2,1)S(1)} %broadcast_in_dim.54), channel_id=1, replica_groups=mesh['leaf'=4,'row'=8,'col'=8] {'col'}, dimensions={0} | all-to-all | bytes 1572864 | tf_op jit(solution)/shard_map/all_to_all | solution.py:33
  302.4 1.6 fusion.31
  303.9 1.9 copy.65
  305.8 3.5 all-to-all-start.15
  309.3 8.3 %all-to-all-done.15 = bf16[8,96,256]{2,1,0:T(8,128)(2,1)S(1)} async-done(((bf16[8,96,256]{2,1,0:T(8,128)(2,1)}), bf16[8,96,256]{2,1,0:T(8,128)(2,1)S(1)}, u32[]{:S(2)}, u32[]{:S(2)}) %all-to-all-start.15) | async-done | bytes 393248 | tf_op jit(solution)/shard_map/all_to_all | solution.py:26
  319.6 4.0 %collective-permute-done.9 = bf16[64,256]{1,0:T(8,128)(2,1)S(1)} collective-permute-done((bf16[64,256]{1,0:T(8,128)(2,1)S(1)}, bf16[64,256]{1,0:T(8,128)(2,1)S(1)}, u32[]{:S(2)}, u32[]{:S(2)}) %collective-permute-start.9) | collective-permute-done | bytes 32800 | tf_op jit(solution)/shard_map/ppermute | solution.py:16
  323.7 11.1 %all_to_all.111 = bf16[8,128,256]{2,1,0:T(8,128)(2,1)S(1)} all-to-all(bf16[8,128,256]{2,1,0:T(8,128)(2,1)S(1)} %broadcast_in_dim.55), channel_id=1, replica_groups=mesh['leaf'=4,'row'=8,'col'=8] {'row'}, dimensions={0} | all-to-all | bytes 1048576 | tf_op jit(solution)/shard_map/all_to_all | solution.py:33
  334.8 2.3 fusion.22
  337.2 12.7 %all_to_all.112 = bf16[8,128,256]{1,2,0:T(8,128)(2,1)S(1)} all-to-all(bf16[8,128,256]{1,2,0:T(8,128)(2,1)S(1)} %bitcast.150), channel_id=1, replica_groups=mesh['leaf'=4,'row'=8,'col'=8] {'col'}, dimensions={0} | all-to-all | bytes 1048576 | tf_op jit(solution)/shard_map/all_to_all | solution.py:26
  350.2 12.8 %all_to_all.113 = bf16[8,128,256]{2,1,0:T(8,128)(2,1)S(1)} all-to-all(bf16[8,128,256]{2,1,0:T(8,128)(2,1)S(1)} %broadcast_in_dim.56), channel_id=1, replica_groups=mesh['leaf'=4,'row'=8,'col'=8] {'col'}, dimensions={0} | all-to-all | bytes 1048576 | tf_op jit(solution)/shard_map/all_to_all | solution.py:33
  363.0 2.3 fusion.28
  365.4 12.4 %all_to_all.114 = bf16[8,128,256]{1,2,0:T(8,128)(2,1)S(1)} all-to-all(bf16[8,128,256]{1,2,0:T(8,128)(2,1)S(1)} %bitcast.151), channel_id=1, replica_groups=mesh['leaf'=4,'row'=8,'col'=8] {'row'}, dimensions={0} | all-to-all | bytes 1048576 | tf_op jit(solution)/shard_map/all_to_all | solution.py:26
  (105 shorter events, 9.0 us)
Async XLA Ops:
  0.6 77.9 %copy-start = (bf16[1536,768]{1,0:T(8,128)(2,1)S(1)}, bf16[1536,768]{1,0:T(8,128)(2,1)}, u32[]{:S(2)}) copy-start(bf16[1536,768]{1,0:T(8,128)(2,1)} %param.15) | copy-start | bytes 7077892
  19.7 26.6 %copy-start.2 = (bf16[1,1024,1024]{2,1,0:T(8,128)(2,1)S(1)}, bf16[1,1024,1024]{2,1,0:T(8,128)(2,1)}, u32[]{:S(2)}) copy-start(bf16[1,1024,1024]{2,1,0:T(8,128)(2,1)} %param.14) | copy-start | bytes 6291460
  46.3 5.1 %copy-start.13 = (s32[1,1,1,2,64]{4,3,2,1,0:T(2,128)S(1)}, s32[1,1,1,2,64]{4,3,2,1,0:T(2,128)}, u32[]{:S(2)}) copy-start(s32[1,1,1,2,64]{4,3,2,1,0:T(2,128)} %param.18) | copy-start | bytes 1540
  47.1 17.4 %copy-start.11 = (f32[1,1,1,96,256]{4,3,2,1,0:T(8,128)S(1)}, f32[1,1,1,96,256]{4,3,2,1,0:T(8,128)}, u32[]{:S(2)}) copy-start(f32[1,1,1,96,256]{4,3,2,1,0:T(8,128)} %param.11) | copy-start | bytes 294916
  47.9 12.9 %all-to-all-start.3 = ((bf16[8,128,256]{1,2,0:T(8,128)(2,1)}), bf16[8,128,256]{1,2,0:T(8,128)(2,1)S(1)}, u32[]{:S(2)}, u32[]{:S(2)}) async-start(bf16[8,128,256]{1,2,0:T(8,128)(2,1)} %bitcast.143), calls=%async_computation.3 | async-start | bytes 1048576 | tf_op jit(solution)/shard_map/all_to_all | solution.py:26
  61.1 5.3 %collective-permute-start = (bf16[64,256]{1,0:T(8,128)(2,1)S(1)}, bf16[64,256]{1,0:T(8,128)(2,1)S(1)}, u32[]{:S(2)}, u32[]{:S(2)}) collective-permute-start(bf16[64,256]{1,0:T(8,128)(2,1)S(1)} %fusion.44), channel_id=1, source_target_pairs={{0,64},{64,0},{128,192},{192,128},{1,65},{65,1},{129,193},{193,129... | collective-permute-start | bytes 98312 | tf_op jit(solution)/shard_map/ppermute | solution.py:16
  67.4 11.1 %copy-start.5 = (f32[160,256]{1,0:T(8,128)}, f32[160,256]{1,0:T(8,128)S(1)}, u32[]{:S(2)}) copy-start(f32[160,256]{1,0:T(8,128)S(1)} %scatter_custom_fusion.1) | copy-start | bytes 491524
  97.2 13.8 %copy-start.12 = (s32[1,1,1,4,16]{4,3,2,1,0:T(4,128)S(1)}, s32[1,1,1,4,16]{4,3,2,1,0:T(4,128)}, u32[]{:S(2)}) copy-start(s32[1,1,1,4,16]{4,3,2,1,0:T(4,128)} %param.19) | copy-start | bytes 772
  97.3 7.8 %collective-permute-start.1 = (bf16[192,256]{1,0:T(8,128)(2,1)S(1)}, bf16[192,256]{1,0:T(8,128)(2,1)S(1)}, u32[]{:S(2)}, u32[]{:S(2)}) collective-permute-start(bf16[192,256]{1,0:T(8,128)(2,1)S(1)} %convert_element_type.203), channel_id=1, source_target_pairs={{0,64},{64,0},{128,192},{192,128},{1,65},{65,1},{129,193},{193,129... | collective-permute-start | bytes 294920 | tf_op jit(solution)/shard_map/ppermute | solution.py:16
  105.2 1.0 copy-start.6
  106.1 16.6 %all-to-all-start.6 = ((bf16[8,192,256]{2,1,0:T(8,128)(2,1)}), bf16[8,192,256]{2,1,0:T(8,128)(2,1)S(1)}, u32[]{:S(2)}, u32[]{:S(2)}) async-start(bf16[8,192,256]{2,1,0:T(8,128)(2,1)} %broadcast_in_dim.49), calls=%async_computation.6 | async-start | bytes 1572864 | tf_op jit(solution)/shard_map/all_to_all | solution.py:33
  122.7 28.7 %copy-start.1 = (f32[1,1,1,64,256]{4,3,2,1,0:T(8,128)S(1)}, f32[1,1,1,64,256]{4,3,2,1,0:T(8,128)}, u32[]{:S(2)}) copy-start(f32[1,1,1,64,256]{4,3,2,1,0:T(8,128)} %param.12) | copy-start | bytes 196612
  127.2 10.6 %all-to-all-start.7 = ((bf16[8,64,256]{2,1,0:T(8,128)(2,1)}), bf16[8,64,256]{2,1,0:T(8,128)(2,1)S(1)}, u32[]{:S(2)}, u32[]{:S(2)}) async-start(bf16[8,64,256]{2,1,0:T(8,128)(2,1)} %bitcast.27), calls=%async_computation.7 | async-start | bytes 524288 | tf_op jit(solution)/shard_map/all_to_all | solution.py:26
  138.7 4.9 %collective-permute-start.2 = (bf16[2,16,256]{2,1,0:T(8,128)(2,1)S(1)}, bf16[2,16,256]{2,1,0:T(8,128)(2,1)S(1)}, u32[]{:S(2)}, u32[]{:S(2)}) collective-permute-start(bf16[2,16,256]{2,1,0:T(8,128)(2,1)S(1)} %pad_maximum_fusion.3), channel_id=1, source_target_pairs={{0,64},{64,0},{128,192},{192,128},{1,65},{65,1},{129,193},{193,129... | collective-permute-start | bytes 49160 | tf_op jit(solution)/shard_map/ppermute | solution.py:16
  143.6 7.7 %collective-permute-start.3 = (bf16[2,16,256]{2,1,0:T(8,128)(2,1)S(1)}, bf16[2,16,256]{2,1,0:T(8,128)(2,1)S(1)}, u32[]{:S(2)}, u32[]{:S(2)}) collective-permute-start(bf16[2,16,256]{2,1,0:T(8,128)(2,1)S(1)} %pad_maximum_fusion.4), channel_id=1, source_target_pairs={{0,128},{128,0},{64,192},{192,64},{1,129},{129,1},{65,193},{193,65... | collective-permute-start | bytes 49160 | tf_op jit(solution)/shard_map/ppermute | solution.py:16
  183.1 8.7 %collective-permute-start.4 = (bf16[256,256]{0,1:T(8,128)(2,1)S(1)}, bf16[256,256]{0,1:T(8,128)(2,1)S(1)}, u32[]{:S(2)}, u32[]{:S(2)}) collective-permute-start(bf16[256,256]{0,1:T(8,128)(2,1)S(1)} %convert_element_type.214), channel_id=1, source_target_pairs={{0,64},{64,0},{128,192},{192,128},{1,65},{65,1},{129,193},{193,129... | collective-permute-start | bytes 393224 | tf_op jit(solution)/shard_map/ppermute | solution.py:16
  191.8 12.2 %collective-permute-start.5 = (bf16[256,256]{0,1:T(8,128)(2,1)S(1)}, bf16[256,256]{0,1:T(8,128)(2,1)S(1)}, u32[]{:S(2)}, u32[]{:S(2)}) collective-permute-start(bf16[256,256]{0,1:T(8,128)(2,1)S(1)} %fusion.34), channel_id=1, source_target_pairs={{0,128},{128,0},{64,192},{192,64},{1,129},{129,1},{65,193},{193,65... | collective-permute-start | bytes 393224 | tf_op jit(solution)/shard_map/ppermute | solution.py:16
  204.1 18.6 %copy-start.3 = (bf16[2048,512]{1,0:T(8,128)(2,1)S(1)}, bf16[2048,512]{1,0:T(8,128)(2,1)}, u32[]{:S(2)}) copy-start(bf16[2048,512]{1,0:T(8,128)(2,1)} %param.17) | copy-start | bytes 6291460
  224.3 10.6 %all-to-all-start.11 = ((bf16[8,64,256]{2,1,0:T(8,128)(2,1)}), bf16[8,64,256]{2,1,0:T(8,128)(2,1)S(1)}, u32[]{:S(2)}, u32[]{:S(2)}) async-start(bf16[8,64,256]{2,1,0:T(8,128)(2,1)} %bitcast.34), calls=%async_computation.11 | async-start | bytes 524288 | tf_op jit(solution)/shard_map/all_to_all | solution.py:26
  234.9 28.7 %copy-start.4 = (f32[64,256]{1,0:T(8,128)}, f32[64,256]{1,0:T(8,128)S(1)}, u32[]{:S(2)}) copy-start(f32[64,256]{1,0:T(8,128)S(1)} %convert_reduce_fusion.8) | copy-start | bytes 196612
  235.6 7.9 %collective-permute-start.6 = (bf16[2,16,256]{2,1,0:T(8,128)(2,1)S(1)}, bf16[2,16,256]{2,1,0:T(8,128)(2,1)S(1)}, u32[]{:S(2)}, u32[]{:S(2)}) collective-permute-start(bf16[2,16,256]{2,1,0:T(8,128)(2,1)S(1)} %pad_maximum_fusion.5), channel_id=1, source_target_pairs={{0,128},{128,0},{64,192},{192,64},{1,129},{129,1},{65,193},{193,65... | collective-permute-start | bytes 49160 | tf_op jit(solution)/shard_map/ppermute | solution.py:16
  243.5 4.8 %collective-permute-start.7 = (bf16[2,16,256]{2,1,0:T(8,128)(2,1)S(1)}, bf16[2,16,256]{2,1,0:T(8,128)(2,1)S(1)}, u32[]{:S(2)}, u32[]{:S(2)}) collective-permute-start(bf16[2,16,256]{2,1,0:T(8,128)(2,1)S(1)} %pad_maximum_fusion.6), channel_id=1, source_target_pairs={{0,64},{64,0},{128,192},{192,128},{1,65},{65,1},{129,193},{193,129... | collective-permute-start | bytes 49160 | tf_op jit(solution)/shard_map/ppermute | solution.py:16
  249.0 0.6 copy-start.9
  263.6 23.1 %copy-start.7 = (bf16[192,256]{1,0:T(8,128)(2,1)S(1)}, bf16[192,256]{1,0:T(8,128)(2,1)}, u32[]{:S(2)}) copy-start(bf16[192,256]{1,0:T(8,128)(2,1)} %copy-done.6) | copy-start | bytes 294916
  279.4 7.3 %collective-permute-start.8 = (bf16[192,256]{1,0:T(8,128)(2,1)S(1)}, bf16[192,256]{1,0:T(8,128)(2,1)S(1)}, u32[]{:S(2)}, u32[]{:S(2)}) collective-permute-start(bf16[192,256]{1,0:T(8,128)(2,1)S(1)} %convert_element_type.227), channel_id=1, source_target_pairs={{0,64},{64,0},{128,192},{192,128},{1,65},{65,1},{129,193},{193,129... | collective-permute-start | bytes 294920 | tf_op jit(solution)/shard_map/ppermute | solution.py:16
  302.4 15.3 %copy-start.10 = (bf16[64,256]{1,0:T(8,128)(2,1)S(1)}, bf16[64,256]{1,0:T(8,128)(2,1)}, u32[]{:S(2)}) copy-start(bf16[64,256]{1,0:T(8,128)(2,1)} %copy-done.9) | copy-start | bytes 98308
  305.8 11.7 %all-to-all-start.15 = ((bf16[8,96,256]{2,1,0:T(8,128)(2,1)}), bf16[8,96,256]{2,1,0:T(8,128)(2,1)S(1)}, u32[]{:S(2)}, u32[]{:S(2)}) async-start(bf16[8,96,256]{2,1,0:T(8,128)(2,1)} %bitcast.45), calls=%async_computation.15 | async-start | bytes 786432 | tf_op jit(solution)/shard_map/all_to_all | solution.py:26
  317.6 6.0 %copy-start.8 = (f32[96,256]{1,0:T(8,128)}, f32[96,256]{1,0:T(8,128)S(1)}, u32[]{:S(2)}) copy-start(f32[96,256]{1,0:T(8,128)S(1)} %convert_reduce_fusion.7) | copy-start | bytes 294916
  318.4 5.3 %collective-permute-start.9 = (bf16[64,256]{1,0:T(8,128)(2,1)S(1)}, bf16[64,256]{1,0:T(8,128)(2,1)S(1)}, u32[]{:S(2)}, u32[]{:S(2)}) collective-permute-start(bf16[64,256]{1,0:T(8,128)(2,1)S(1)} %gather_fusion.4), channel_id=1, source_target_pairs={{0,64},{64,0},{128,192},{192,128},{1,65},{65,1},{129,193},{193,129... | collective-permute-start | bytes 98312 | tf_op jit(solution)/shard_map/ppermute | solution.py:16

commit v3 on v2

--- a/solution.py
+++ b/solution.py
@@ -38,8 +38,14 @@
     result = scatter_sum(
         jnp.dot(matrix, gathered, preferred_element_type=jnp.float32), "col", jnp.bfloat16
     )
-    for leaf_bit in leaf_bits:
-        result = result + partner(result, leaf_bit)
+    if len(leaf_bits) == 1:
+        result = result + partner(result, leaf_bits[0])
+    elif leaf_bits:
+        count = lax.axis_size("leaf")
+        copies = jnp.broadcast_to(result.astype(jnp.bfloat16)[None], (count,) + result.shape)
+        others = lax.all_to_all(copies, "leaf", 0, 0, tiled=True).astype(jnp.float32)
+        own = jnp.arange(count) == lax.axis_index("leaf")
+        result = result + jnp.where(own[:, None, None], 0.0, others).sum(0)
     return result
 
 
@@ -89,8 +95,6 @@
     own_half = group_id % 2
     child_slots = parent_slot(rows_low.reshape(2, -1), pivot_local, update_local)
     root_slots = rows_mid.reshape(4, -1) % top_local
-    source_order = jnp.bitwise_xor(group_id, jnp.arange(4, dtype=jnp.int32))
-    source_slots = jnp.take(root_slots, source_order, axis=0).reshape(-1)
     own_slots = pick_span(child_slots, own_half)
     other_slots = pick_span(child_slots, 1 - own_half)
     low_y = forward_apply(pivot_local_low, low_in.astype(jnp.bfloat16), ())
@@ -101,31 +105,14 @@
     front_rows = front_rows.at[own_slots].add(-own_part).at[other_slots].add(-came_part)
     mid_y = forward_apply(pivot_mid, front_rows[:pivot_local].astype(jnp.bfloat16), (0,))
     mid_c = front_rows[pivot_local:] - reverse_apply(update_mid, mid_y.astype(jnp.bfloat16))
-    spans = mid_c.reshape(4, -1, rhs_width)
-    kept_spans = jnp.stack(
-        [pick_span(spans, group_id), pick_span(spans, jnp.bitwise_xor(group_id, 2))]
-    )
-    moved_spans = partner(
-        jnp.stack(
-            [
-                pick_span(spans, jnp.bitwise_xor(group_id, 1)),
-                pick_span(spans, jnp.bitwise_xor(group_id, 3)),
-            ]
-        ),
-        0,
-    )
-    second = partner(jnp.stack([kept_spans[1], moved_spans[1]]), 1)
-    arrived = jnp.stack([kept_spans[0], moved_spans[0], second[0], second[1]]).reshape(
-        -1, rhs_width
-    )
-    top_front = top_in.at[source_slots].add(arrived)
+    spans = mid_c.reshape(4, -1, rhs_width).astype(jnp.bfloat16)
+    arrived = lax.all_to_all(spans, "leaf", 0, 0, tiled=True).astype(jnp.float32)
+    top_front = top_in.at[root_slots.reshape(-1)].add(arrived.reshape(-1, rhs_width))
     top_y = forward_apply(pivot_top, top_front.astype(jnp.bfloat16), (0, 1))
     top_x = reverse_apply(pivot_top, top_y.astype(jnp.bfloat16))
-    asked_rows = top_x[source_slots].reshape(4, -1, rhs_width)
-    back_one = partner(jnp.stack([asked_rows[2], asked_rows[3]]), 1)
-    back_zero = partner(jnp.stack([asked_rows[1], back_one[1]]), 0)
-    by_root = jnp.stack([asked_rows[0], back_zero[0], back_one[0], back_zero[1]])
-    mid_above = jnp.take(by_root, source_order, axis=0).reshape(-1, rhs_width)
+    asked_rows = top_x[root_slots.reshape(-1)].reshape(4, -1, rhs_width).astype(jnp.bfloat16)
+    mid_above = lax.all_to_all(asked_rows, "leaf", 0, 0, tiled=True).astype(jnp.float32)
+    mid_above = mid_above.reshape(-1, rhs_width)
     mid_sum = forward_apply(update_mid, mid_above.astype(jnp.bfloat16), (0,))
     mid_x = reverse_apply(pivot_mid, (mid_y - mid_sum).astype(jnp.bfloat16))
     front_values = jnp.concatenate([mid_x, mid_above], 0)

time: 380 us -> 374 us (0.984)
  blocking collectives: 205 us -> 232 us
  starting transfers between devices: 46.4 us -> 32.3 us
  waiting for transfers between devices: 84.9 us -> 71.4 us
    ppermute x10 -> x4, waiting for transfers between devices: 42 us -> 16.3 us  [from_partner(): return lax.ppermute(block, axis, route)]
    ppermute x10 -> x4, starting transfers between devices: 27.8 us -> 7.64 us  [from_partner(): return lax.ppermute(block, axis, route)]
    all_to_all x9 -> x10, blocking collectives: 117 us -> 133 us  [gather_rows(): lax.all_to_all(copies, axis, 0, 0, tiled=True).reshape(-1, block.shape[-1])]
    all_to_all x1 -> x2, waiting for transfers between devices: 11.7 us -> 23.1 us  [the longest x1 15.2 us: forward_apply(): lax.all_to_all(copies, 'leaf', 0, 0, tiled=True).astype(jnp.float32)]
    all_to_all x0 -> x1, blocking collectives: none -> 10.7 us  [body(): lax.all_to_all(asked_rows, 'leaf', 0, 0, tiled=True).astype(jnp.float32)]
    all_to_all x1 -> x2, starting transfers between devices: 4.87 us -> 10 us  [the longest x1 6.58 us: body(): lax.all_to_all(spans, 'leaf', 0, 0, tiled=True).astype(jnp.float32)]
  transfers between devices with their start and end apart: 15 -> 10, of which waited for: 15 -> 10; matrix products, arithmetic and copies ran while one was open for 1% -> 1% of each run, Pallas kernels for 0% -> 0%
where the time goes in v3:
time: 374 us; the launch traced here: 373 us
  blocking collectives  232 us (62%)
  waiting for transfers between devices  71.4 us (19%)
  starting transfers between devices  32.3 us (9%)
  matrix products  16.8 us (4%)
  local copies, waits for them, and re-layouts  12.8 us (3%)
  other arithmetic  6.61 us (2%)
    all_to_all x10, blocking collectives, gather_rows(): lax.all_to_all(copies, axis, 0, 0, tiled=True).reshape(-1, block.shape[-1])  133 us
    all_to_all x6, blocking collectives, scatter_sum(): pieces = lax.all_to_all(pieces, axis, 0, 0, tiled=True)  88.5 us
    all_to_all x4, waiting for transfers between devices, scatter_sum(): pieces = lax.all_to_all(pieces, axis, 0, 0, tiled=True)  31.9 us
    ppermute x4, waiting for transfers between devices, from_partner(): return lax.ppermute(block, axis, route)  16.3 us
    all_to_all x1, waiting for transfers between devices, forward_apply(): lax.all_to_all(copies, 'leaf', 0, 0, tiled=True).astype(jnp.float32)  15.2 us
    all_to_all x4, starting transfers between devices, scatter_sum(): pieces = lax.all_to_all(pieces, axis, 0, 0, tiled=True)  14.6 us
    dot_general x5, matrix products, forward_apply(): jnp.dot(matrix, gathered, preferred_element_type=jnp.float32)  11.6 us
    all_to_all x1, blocking collectives, body(): lax.all_to_all(asked_rows, 'leaf', 0, 0, tiled=True).astype(jnp.float32)  10.7 us
  transfers between devices with their start and end apart: 10, of which 10 were waited for; matrix products, arithmetic and copies ran while one was open for 1% of the time, Pallas kernels for 0%

profile of v3, /device:TPU:2, one launch (start us, length us, event | category | flops | bytes accessed | tf_op | source)
XLA Modules:
  0.0 372.8 jit_solution(852056522555280695)
XLA Ops:
  0.6 1.1 convert_bitcast_fusion
  1.7 15.7 %all_to_all.115 = bf16[8,128,256]{2,1,0:T(8,128)(2,1)S(1)} all-to-all(bf16[8,128,256]{2,1,0:T(8,128)(2,1)S(1)} %broadcast_in_dim.30), channel_id=1, replica_groups=mesh['leaf'=4,'row'=8,'col'=8] {'row'}, dimensions={0} | all-to-all | bytes 1048576 | tf_op jit(solution)/shard_map/all_to_all | solution.py:33
  17.4 2.3 fusion.10
  19.8 13.7 %all_to_all.116 = bf16[8,128,256]{2,1,0:T(8,128)(2,1)S(1)} all-to-all(bf16[8,128,256]{2,1,0:T(8,128)(2,1)S(1)} %bitcast.149), channel_id=1, replica_groups=mesh['leaf'=4,'row'=8,'col'=8] {'col'}, dimensions={0} | all-to-all | bytes 1048576 | tf_op jit(solution)/shard_map/all_to_all | solution.py:26
  33.5 12.8 %all_to_all.117 = bf16[8,128,256]{2,1,0:T(8,128)(2,1)S(1)} all-to-all(bf16[8,128,256]{2,1,0:T(8,128)(2,1)S(1)} %broadcast_in_dim.31), channel_id=1, replica_groups=mesh['leaf'=4,'row'=8,'col'=8] {'col'}, dimensions={0} | all-to-all | bytes 1048576 | tf_op jit(solution)/shard_map/all_to_all | solution.py:33
  46.3 0.7 fusion.25
  47.1 0.9 copy.109
  48.0 3.5 all-to-all-start.3
  51.5 9.4 %all-to-all-done.3 = bf16[8,128,256]{1,2,0:T(8,128)(2,1)S(1)} async-done(((bf16[8,128,256]{1,2,0:T(8,128)(2,1)}), bf16[8,128,256]{1,2,0:T(8,128)(2,1)S(1)}, u32[]{:S(2)}, u32[]{:S(2)}) %all-to-all-start.3) | async-done | bytes 524320 | tf_op jit(solution)/shard_map/all_to_all | solution.py:26
  61.1 3.4 collective-permute-start
  64.5 1.0 scatter_custom_fusion
  65.5 0.8 collective-permute-done
  66.3 1.0 scatter_custom_fusion.1
  67.4 11.1 %all_to_all.118 = bf16[8,96,256]{2,1,0:T(8,128)(2,1)S(1)} all-to-all(bf16[8,96,256]{2,1,0:T(8,128)(2,1)S(1)} %broadcast_in_dim.32), channel_id=1, replica_groups=mesh['leaf'=4,'row'=8,'col'=8] {'row'}, dimensions={0} | all-to-all | bytes 786432 | tf_op jit(solution)/shard_map/all_to_all | solution.py:33
  78.5 1.7 fusion.1
  80.2 1.4 copy.78
  81.6 15.6 %all_to_all.119 = bf16[8,192,256]{2,1,0:T(8,128)(2,1)S(1)} all-to-all(bf16[8,192,256]{2,1,0:T(8,128)(2,1)S(1)} %bitcast.135), channel_id=1, replica_groups=mesh['leaf'=4,'row'=8,'col'=8] {'col'}, dimensions={0} | all-to-all | bytes 1572864 | tf_op jit(solution)/shard_map/all_to_all | solution.py:26
  97.3 3.3 collective-permute-start.1
  100.6 4.5 %collective-permute-done.1 = bf16[192,256]{1,0:T(8,128)(2,1)S(1)} collective-permute-done((bf16[192,256]{1,0:T(8,128)(2,1)S(1)}, bf16[192,256]{1,0:T(8,128)(2,1)S(1)}, u32[]{:S(2)}, u32[]{:S(2)}) %collective-permute-start.1) | collective-permute-done | bytes 98336 | tf_op jit(solution)/shard_map/ppermute | solution.py:16
  105.2 15.6 %all_to_all.120 = bf16[8,192,256]{2,1,0:T(8,128)(2,1)S(1)} all-to-all(bf16[8,192,256]{2,1,0:T(8,128)(2,1)S(1)} %broadcast_in_dim.37), channel_id=1, replica_groups=mesh['leaf'=4,'row'=8,'col'=8] {'col'}, dimensions={0} | all-to-all | bytes 1572864 | tf_op jit(solution)/shard_map/all_to_all | solution.py:33
  121.4 0.8 copy.79
  122.3 3.4 all-to-all-start.7
  125.8 7.1 %all-to-all-done.7 = bf16[8,64,256]{2,1,0:T(8,128)(2,1)S(1)} async-done(((bf16[8,64,256]{2,1,0:T(8,128)(2,1)}), bf16[8,64,256]{2,1,0:T(8,128)(2,1)S(1)}, u32[]{:S(2)}, u32[]{:S(2)}) %all-to-all-start.7) | async-done | bytes 262176 | tf_op jit(solution)/shard_map/all_to_all | solution.py:26
  132.9 0.6 fusion.36
  133.5 6.6 %all-to-all-start.8 = ((bf16[4,16,256]{2,1,0:T(8,128)(2,1)}), bf16[4,16,256]{2,1,0:T(8,128)(2,1)S(1)}, u32[]{:S(2)}, u32[]{:S(2)}) async-start(bf16[4,16,256]{2,1,0:T(8,128)(2,1)} %bitcast.26), calls=%async_computation.8 | async-start | bytes 65536 | tf_op jit(solution)/shard_map/all_to_all | solution.py:109
  140.1 7.9 %all-to-all-done.8 = bf16[4,16,256]{2,1,0:T(8,128)(2,1)S(1)} async-done(((bf16[4,16,256]{2,1,0:T(8,128)(2,1)}), bf16[4,16,256]{2,1,0:T(8,128)(2,1)S(1)}, u32[]{:S(2)}, u32[]{:S(2)}) %all-to-all-start.8) | async-done | bytes 32800 | tf_op jit(solution)/shard_map/all_to_all | solution.py:109
  147.9 1.0 scatter_custom_fusion.2
  149.0 9.8 %all_to_all.121 = bf16[8,64,256]{2,1,0:T(8,128)(2,1)S(1)} all-to-all(bf16[8,64,256]{2,1,0:T(8,128)(2,1)S(1)} %broadcast_in_dim.38), channel_id=1, replica_groups=mesh['leaf'=4,'row'=8,'col'=8] {'row'}, dimensions={0} | all-to-all | bytes 524288 | tf_op jit(solution)/shard_map/all_to_all | solution.py:33
  158.8 2.4 convolution_convert_fusion
  161.2 18.4 %all_to_all.122 = bf16[8,256,256]{1,2,0:T(8,128)(2,1)S(1)} all-to-all(bf16[8,256,256]{1,2,0:T(8,128)(2,1)S(1)} %bitcast.134), channel_id=1, replica_groups=mesh['leaf'=4,'row'=8,'col'=8] {'col'}, dimensions={0} | all-to-all | bytes 2097152 | tf_op jit(solution)/shard_map/all_to_all | solution.py:26
  179.9 0.8 broadcast_in_dim.41
  180.7 3.5 all-to-all-start.11
  184.2 15.2 %all-to-all-done.11 = bf16[4,256,256]{2,1,0:T(8,128)(2,1)S(1)} async-done(((bf16[4,256,256]{2,1,0:T(8,128)(2,1)}), bf16[4,256,256]{2,1,0:T(8,128)(2,1)S(1)}, u32[]{:S(2)}, u32[]{:S(2)}) %all-to-all-start.11) | async-done | bytes 524320 | tf_op jit(solution)/shard_map/all_to_all | solution.py:46
  199.5 0.9 select_reduce_fusion
  200.3 1.1 copy.83
  201.7 18.5 %all_to_all.123 = bf16[8,256,256]{2,1,0:T(8,128)(2,1)S(1)} all-to-all(bf16[8,256,256]{2,1,0:T(8,128)(2,1)S(1)} %broadcast_in_dim.42), channel_id=1, replica_groups=mesh['leaf'=4,'row'=8,'col'=8] {'col'}, dimensions={0} | all-to-all | bytes 2097152 | tf_op jit(solution)/shard_map/all_to_all | solution.py:33
  220.2 0.7 fusion.33
  220.9 0.8 copy.85
  221.8 4.2 %all-to-all-start.13 = ((bf16[8,64,256]{2,1,0:T(8,128)(2,1)}), bf16[8,64,256]{2,1,0:T(8,128)(2,1)S(1)}, u32[]{:S(2)}, u32[]{:S(2)}) async-start(bf16[8,64,256]{2,1,0:T(8,128)(2,1)} %bitcast.32), calls=%async_computation.13 | async-start | bytes 524288 | tf_op jit(solution)/shard_map/all_to_all | solution.py:26
  226.0 7.2 %all-to-all-done.13 = bf16[8,64,256]{2,1,0:T(8,128)(2,1)S(1)} async-done(((bf16[8,64,256]{2,1,0:T(8,128)(2,1)}), bf16[8,64,256]{2,1,0:T(8,128)(2,1)S(1)}, u32[]{:S(2)}, u32[]{:S(2)}) %all-to-all-start.13) | async-done | bytes 262176 | tf_op jit(solution)/shard_map/all_to_all | solution.py:26
  233.2 0.7 gather_fusion
  233.9 10.7 %all_to_all.124 = bf16[4,16,256]{2,1,0:T(8,128)(2,1)S(1)} all-to-all(bf16[4,16,256]{2,1,0:T(8,128)(2,1)S(1)} %bitcast.159), channel_id=1, replica_groups=mesh['leaf'=4,'row'=8,'col'=8] {'leaf'}, dimensions={0} | all-to-all | bytes 65536 | tf_op jit(solution)/shard_map/all_to_all | solution.py:114
  244.6 0.6 copy-done.8
  245.2 9.8 %all_to_all.125 = bf16[8,64,256]{2,1,0:T(8,128)(2,1)S(1)} all-to-all(bf16[8,64,256]{2,1,0:T(8,128)(2,1)S(1)} %broadcast_in_dim.43), channel_id=1, replica_groups=mesh['leaf'=4,'row'=8,'col'=8] {'row'}, dimensions={0} | all-to-all | bytes 524288 | tf_op jit(solution)/shard_map/all_to_all | solution.py:33
  255.0 2.9 fusion
  257.9 1.4 copy.86
  259.3 15.7 %all_to_all.126 = bf16[8,192,256]{2,1,0:T(8,128)(2,1)S(1)} all-to-all(bf16[8,192,256]{2,1,0:T(8,128)(2,1)S(1)} %bitcast.136), channel_id=1, replica_groups=mesh['leaf'=4,'row'=8,'col'=8] {'col'}, dimensions={0} | all-to-all | bytes 1572864 | tf_op jit(solution)/shard_map/all_to_all | solution.py:26
  275.1 0.9 collective-permute-start.2
  276.0 6.5 %collective-permute-done.2 = bf16[192,256]{1,0:T(8,128)(2,1)S(1)} collective-permute-done((bf16[192,256]{1,0:T(8,128)(2,1)S(1)}, bf16[192,256]{1,0:T(8,128)(2,1)S(1)}, u32[]{:S(2)}, u32[]{:S(2)}) %collective-permute-start.2) | collective-permute-done | bytes 98336 | tf_op jit(solution)/shard_map/ppermute | solution.py:16
  282.7 15.6 %all_to_all.127 = bf16[8,192,256]{2,1,0:T(8,128)(2,1)S(1)} all-to-all(bf16[8,192,256]{2,1,0:T(8,128)(2,1)S(1)} %broadcast_in_dim.44), channel_id=1, replica_groups=mesh['leaf'=4,'row'=8,'col'=8] {'col'}, dimensions={0} | all-to-all | bytes 1572864 | tf_op jit(solution)/shard_map/all_to_all | solution.py:33
  298.3 0.8 fusion.31
  299.1 0.9 copy.87
  300.0 3.5 all-to-all-start.18
  303.5 8.3 %all-to-all-done.18 = bf16[8,96,256]{2,1,0:T(8,128)(2,1)S(1)} async-done(((bf16[8,96,256]{2,1,0:T(8,128)(2,1)}), bf16[8,96,256]{2,1,0:T(8,128)(2,1)S(1)}, u32[]{:S(2)}, u32[]{:S(2)}) %all-to-all-start.18) | async-done | bytes 393248 | tf_op jit(solution)/shard_map/all_to_all | solution.py:26
  311.8 0.7 gather_fusion.2
  312.7 0.7 gather_fusion.1
  313.4 4.4 %collective-permute-done.3 = bf16[64,256]{1,0:T(8,128)(2,1)S(1)} collective-permute-done((bf16[64,256]{1,0:T(8,128)(2,1)S(1)}, bf16[64,256]{1,0:T(8,128)(2,1)S(1)}, u32[]{:S(2)}, u32[]{:S(2)}) %collective-permute-start.3) | collective-permute-done | bytes 32800 | tf_op jit(solution)/shard_map/ppermute | solution.py:16
  317.9 11.1 %all_to_all.128 = bf16[8,128,256]{2,1,0:T(8,128)(2,1)S(1)} all-to-all(bf16[8,128,256]{2,1,0:T(8,128)(2,1)S(1)} %broadcast_in_dim.45), channel_id=1, replica_groups=mesh['leaf'=4,'row'=8,'col'=8] {'row'}, dimensions={0} | all-to-all | bytes 1048576 | tf_op jit(solution)/shard_map/all_to_all | solution.py:33
  328.9 2.4 fusion.22
  331.4 12.7 %all_to_all.129 = bf16[8,128,256]{1,2,0:T(8,128)(2,1)S(1)} all-to-all(bf16[8,128,256]{1,2,0:T(8,128)(2,1)S(1)} %bitcast.138), channel_id=1, replica_groups=mesh['leaf'=4,'row'=8,'col'=8] {'col'}, dimensions={0} | all-to-all | bytes 1048576 | tf_op jit(solution)/shard_map/all_to_all | solution.py:26
  344.4 12.8 %all_to_all.130 = bf16[8,128,256]{2,1,0:T(8,128)(2,1)S(1)} all-to-all(bf16[8,128,256]{2,1,0:T(8,128)(2,1)S(1)} %broadcast_in_dim.46), channel_id=1, replica_groups=mesh['leaf'=4,'row'=8,'col'=8] {'col'}, dimensions={0} | all-to-all | bytes 1048576 | tf_op jit(solution)/shard_map/all_to_all | solution.py:33
  357.1 2.3 fusion.28
  359.6 12.4 %all_to_all.131 = bf16[8,128,256]{1,2,0:T(8,128)(2,1)S(1)} all-to-all(bf16[8,128,256]{1,2,0:T(8,128)(2,1)S(1)} %bitcast.139), channel_id=1, replica_groups=mesh['leaf'=4,'row'=8,'col'=8] {'row'}, dimensions={0} | all-to-all | bytes 1048576 | tf_op jit(solution)/shard_map/all_to_all | solution.py:26
  372.0 0.8 copy.93
  (78 shorter events, 2.9 us)
Async XLA Ops:
  0.6 77.9 %copy-start = (bf16[1536,768]{1,0:T(8,128)(2,1)S(1)}, bf16[1536,768]{1,0:T(8,128)(2,1)}, u32[]{:S(2)}) copy-start(bf16[1536,768]{1,0:T(8,128)(2,1)} %param.15) | copy-start | bytes 7077892
  19.7 26.6 %copy-start.2 = (bf16[1,1024,1024]{2,1,0:T(8,128)(2,1)S(1)}, bf16[1,1024,1024]{2,1,0:T(8,128)(2,1)}, u32[]{:S(2)}) copy-start(bf16[1,1024,1024]{2,1,0:T(8,128)(2,1)} %param.14) | copy-start | bytes 6291460
  46.3 5.2 %copy-start.13 = (s32[1,1,1,2,64]{4,3,2,1,0:T(2,128)S(1)}, s32[1,1,1,2,64]{4,3,2,1,0:T(2,128)}, u32[]{:S(2)}) copy-start(s32[1,1,1,2,64]{4,3,2,1,0:T(2,128)} %param.18) | copy-start | bytes 1540
  47.1 17.4 %copy-start.11 = (f32[1,1,1,96,256]{4,3,2,1,0:T(8,128)S(1)}, f32[1,1,1,96,256]{4,3,2,1,0:T(8,128)}, u32[]{:S(2)}) copy-start(f32[1,1,1,96,256]{4,3,2,1,0:T(8,128)} %param.11) | copy-start | bytes 294916
  48.0 12.9 %all-to-all-start.3 = ((bf16[8,128,256]{1,2,0:T(8,128)(2,1)}), bf16[8,128,256]{1,2,0:T(8,128)(2,1)S(1)}, u32[]{:S(2)}, u32[]{:S(2)}) async-start(bf16[8,128,256]{1,2,0:T(8,128)(2,1)} %bitcast.132), calls=%async_computation.3 | async-start | bytes 1048576 | tf_op jit(solution)/shard_map/all_to_all | solution.py:26
  61.1 5.3 %collective-permute-start = (bf16[64,256]{1,0:T(8,128)(2,1)S(1)}, bf16[64,256]{1,0:T(8,128)(2,1)S(1)}, u32[]{:S(2)}, u32[]{:S(2)}) collective-permute-start(bf16[64,256]{1,0:T(8,128)(2,1)S(1)} %fusion.46), channel_id=1, source_target_pairs={{0,64},{64,0},{128,192},{192,128},{1,65},{65,1},{129,193},{193,129... | collective-permute-start | bytes 98312 | tf_op jit(solution)/shard_map/ppermute | solution.py:16
  97.2 23.6 %copy-start.1 = (bf16[1536,512]{1,0:T(8,128)(2,1)S(1)}, bf16[1536,512]{1,0:T(8,128)(2,1)}, u32[]{:S(2)}) copy-start(bf16[1536,512]{1,0:T(8,128)(2,1)} %param.16) | copy-start | bytes 4718596
  97.3 7.8 %collective-permute-start.1 = (bf16[192,256]{1,0:T(8,128)(2,1)S(1)}, bf16[192,256]{1,0:T(8,128)(2,1)S(1)}, u32[]{:S(2)}, u32[]{:S(2)}) collective-permute-start(bf16[192,256]{1,0:T(8,128)(2,1)S(1)} %convert_element_type.205), channel_id=1, source_target_pairs={{0,64},{64,0},{128,192},{192,128},{1,65},{65,1},{129,193},{193,129... | collective-permute-start | bytes 294920 | tf_op jit(solution)/shard_map/ppermute | solution.py:16
  105.1 15.7 %copy-start.5 = (bf16[192,256]{1,0:T(8,128)(2,1)}, bf16[192,256]{1,0:T(8,128)(2,1)S(1)}, u32[]{:S(2)}) copy-start(bf16[192,256]{1,0:T(8,128)(2,1)S(1)} %collective-permute-done.1) | copy-start | bytes 294916
  120.8 4.9 %copy-start.12 = (s32[1,1,1,4,16]{4,3,2,1,0:T(4,128)S(1)}, s32[1,1,1,4,16]{4,3,2,1,0:T(4,128)}, u32[]{:S(2)}) copy-start(s32[1,1,1,4,16]{4,3,2,1,0:T(4,128)} %param.19) | copy-start | bytes 772
  120.8 27.1 %copy-start.10 = (f32[1,1,1,64,256]{4,3,2,1,0:T(8,128)S(1)}, f32[1,1,1,64,256]{4,3,2,1,0:T(8,128)}, u32[]{:S(2)}) copy-start(f32[1,1,1,64,256]{4,3,2,1,0:T(8,128)} %param.12) | copy-start | bytes 196612
  122.3 10.6 %all-to-all-start.7 = ((bf16[8,64,256]{2,1,0:T(8,128)(2,1)}), bf16[8,64,256]{2,1,0:T(8,128)(2,1)S(1)}, u32[]{:S(2)}, u32[]{:S(2)}) async-start(bf16[8,64,256]{2,1,0:T(8,128)(2,1)} %bitcast.25), calls=%async_computation.7 | async-start | bytes 524288 | tf_op jit(solution)/shard_map/all_to_all | solution.py:26
  133.5 14.4 %all-to-all-start.8 = ((bf16[4,16,256]{2,1,0:T(8,128)(2,1)}), bf16[4,16,256]{2,1,0:T(8,128)(2,1)S(1)}, u32[]{:S(2)}, u32[]{:S(2)}) async-start(bf16[4,16,256]{2,1,0:T(8,128)(2,1)} %bitcast.26), calls=%async_computation.8 | async-start | bytes 65536 | tf_op jit(solution)/shard_map/all_to_all | solution.py:109
  180.7 18.7 %all-to-all-start.11 = ((bf16[4,256,256]{2,1,0:T(8,128)(2,1)}), bf16[4,256,256]{2,1,0:T(8,128)(2,1)S(1)}, u32[]{:S(2)}, u32[]{:S(2)}) async-start(bf16[4,256,256]{2,1,0:T(8,128)(2,1)} %broadcast_in_dim.41), calls=%async_computation.11 | async-start | bytes 1048576 | tf_op jit(solution)/shard_map/all_to_all | solution.py:46
  201.6 18.6 %copy-start.3 = (bf16[2048,512]{1,0:T(8,128)(2,1)S(1)}, bf16[2048,512]{1,0:T(8,128)(2,1)}, u32[]{:S(2)}) copy-start(bf16[2048,512]{1,0:T(8,128)(2,1)} %param.17) | copy-start | bytes 6291460
  221.8 11.4 %all-to-all-start.13 = ((bf16[8,64,256]{2,1,0:T(8,128)(2,1)}), bf16[8,64,256]{2,1,0:T(8,128)(2,1)S(1)}, u32[]{:S(2)}, u32[]{:S(2)}) async-start(bf16[8,64,256]{2,1,0:T(8,128)(2,1)} %bitcast.32), calls=%async_computation.13 | async-start | bytes 524288 | tf_op jit(solution)/shard_map/all_to_all | solution.py:26
  233.2 26.1 %copy-start.4 = (f32[64,256]{1,0:T(8,128)}, f32[64,256]{1,0:T(8,128)S(1)}, u32[]{:S(2)}) copy-start(f32[64,256]{1,0:T(8,128)S(1)} %convert_reduce_fusion.8) | copy-start | bytes 196612
  244.6 0.6 copy-start.8
  259.3 23.3 %copy-start.6 = (bf16[192,256]{1,0:T(8,128)(2,1)S(1)}, bf16[192,256]{1,0:T(8,128)(2,1)}, u32[]{:S(2)}) copy-start(bf16[192,256]{1,0:T(8,128)(2,1)} %copy-done.5) | copy-start | bytes 294916
  275.1 7.4 %collective-permute-start.2 = (bf16[192,256]{1,0:T(8,128)(2,1)S(1)}, bf16[192,256]{1,0:T(8,128)(2,1)S(1)}, u32[]{:S(2)}, u32[]{:S(2)}) collective-permute-start(bf16[192,256]{1,0:T(8,128)(2,1)S(1)} %convert_element_type.228), channel_id=1, source_target_pairs={{0,64},{64,0},{128,192},{192,128},{1,65},{65,1},{129,193},{193,129... | collective-permute-start | bytes 294920 | tf_op jit(solution)/shard_map/ppermute | solution.py:16
  298.3 13.5 %copy-start.9 = (bf16[4,16,256]{2,1,0:T(8,128)(2,1)S(1)}, bf16[4,16,256]{2,1,0:T(8,128)(2,1)}, u32[]{:S(2)}) copy-start(bf16[4,16,256]{2,1,0:T(8,128)(2,1)} %copy-done.8) | copy-start | bytes 98308
  300.0 11.7 %all-to-all-start.18 = ((bf16[8,96,256]{2,1,0:T(8,128)(2,1)}), bf16[8,96,256]{2,1,0:T(8,128)(2,1)S(1)}, u32[]{:S(2)}, u32[]{:S(2)}) async-start(bf16[8,96,256]{2,1,0:T(8,128)(2,1)} %bitcast.40), calls=%async_computation.18 | async-start | bytes 786432 | tf_op jit(solution)/shard_map/all_to_all | solution.py:26
  311.8 19.5 %copy-start.7 = (f32[96,256]{1,0:T(8,128)}, f32[96,256]{1,0:T(8,128)S(1)}, u32[]{:S(2)}) copy-start(f32[96,256]{1,0:T(8,128)S(1)} %convert_reduce_fusion.7) | copy-start | bytes 294916
  312.5 5.3 %collective-permute-start.3 = (bf16[64,256]{1,0:T(8,128)(2,1)S(1)}, bf16[64,256]{1,0:T(8,128)(2,1)S(1)}, u32[]{:S(2)}, u32[]{:S(2)}) collective-permute-start(bf16[64,256]{1,0:T(8,128)(2,1)S(1)} %gather_fusion.2), channel_id=1, source_target_pairs={{0,64},{64,0},{128,192},{192,128},{1,65},{65,1},{129,193},{193,129... | collective-permute-start | bytes 98312 | tf_op jit(solution)/shard_map/ppermute | solution.py:16

commit v4 on v3

--- a/solution.py
+++ b/solution.py
@@ -14,6 +14,17 @@
         if high != low and high < count:
             route += [(low, high), (high, low)]
     return lax.ppermute(block, axis, route)
+
+
+def leaf_exchange(blocks):
+    group = lax.axis_index("leaf")
+    count = lax.axis_size("leaf")
+    came = [pick_span(blocks, group)]
+    for step in range(1, count):
+        route = [(low, low ^ step) for low in range(count)]
+        came.append(lax.ppermute(pick_span(blocks, group ^ step), "leaf", route))
+    order = jnp.bitwise_xor(jnp.arange(count, dtype=jnp.int32), group)
+    return jnp.take(jnp.stack(came), order, axis=0)
 
 
 def partner(block_data, leaf_bit):
@@ -42,10 +53,12 @@
         result = result + partner(result, leaf_bits[0])
     elif leaf_bits:
         count = lax.axis_size("leaf")
-        copies = jnp.broadcast_to(result.astype(jnp.bfloat16)[None], (count,) + result.shape)
-        others = lax.all_to_all(copies, "leaf", 0, 0, tiled=True).astype(jnp.float32)
-        own = jnp.arange(count) == lax.axis_index("leaf")
-        result = result + jnp.where(own[:, None, None], 0.0, others).sum(0)
+        sent = result.astype(jnp.bfloat16)
+        total = result
+        for step in range(1, count):
+            route = [(low, low ^ step) for low in range(count)]
+            total = total + lax.ppermute(sent, "leaf", route).astype(jnp.float32)
+        result = total
     return result
 
 
@@ -106,12 +119,12 @@
     mid_y = forward_apply(pivot_mid, front_rows[:pivot_local].astype(jnp.bfloat16), (0,))
     mid_c = front_rows[pivot_local:] - reverse_apply(update_mid, mid_y.astype(jnp.bfloat16))
     spans = mid_c.reshape(4, -1, rhs_width).astype(jnp.bfloat16)
-    arrived = lax.all_to_all(spans, "leaf", 0, 0, tiled=True).astype(jnp.float32)
+    arrived = leaf_exchange(spans).astype(jnp.float32)
     top_front = top_in.at[root_slots.reshape(-1)].add(arrived.reshape(-1, rhs_width))
     top_y = forward_apply(pivot_top, top_front.astype(jnp.bfloat16), (0, 1))
     top_x = reverse_apply(pivot_top, top_y.astype(jnp.bfloat16))
     asked_rows = top_x[root_slots.reshape(-1)].reshape(4, -1, rhs_width).astype(jnp.bfloat16)
-    mid_above = lax.all_to_all(asked_rows, "leaf", 0, 0, tiled=True).astype(jnp.float32)
+    mid_above = leaf_exchange(asked_rows).astype(jnp.float32)
     mid_above = mid_above.reshape(-1, rhs_width)
     mid_sum = forward_apply(update_mid, mid_above.astype(jnp.bfloat16), (0,))
     mid_x = reverse_apply(pivot_mid, (mid_y - mid_sum).astype(jnp.bfloat16))

time: 374 us -> 367 us (0.981)
  blocking collectives: 232 us -> 221 us
  starting transfers between devices: 32.3 us -> 42.2 us
  waiting for transfers between devices: 71.4 us -> 66.8 us
    all_to_all x2 -> x0, waiting for transfers between devices: 23.1 us -> none  [the longest x1 15.2 us: forward_apply(): lax.all_to_all(copies, 'leaf', 0, 0, tiled=True).astype(jnp.float32)]
    ppermute x0 -> x9, starting transfers between devices: none -> 19.8 us  [the longest x6 13.2 us: leaf_exchange(): came.append(lax.ppermute(pick_span(blocks, group ^ step), 'leaf', route))]
    ppermute x0 -> x9, waiting for transfers between devices: none -> 18.9 us  [the longest x3 10 us: forward_apply(): total = total + lax.ppermute(sent, 'leaf', route).astype(jnp.float32)]
    all_to_all x1 -> x0, blocking collectives: 10.7 us -> none  [body(): lax.all_to_all(asked_rows, 'leaf', 0, 0, tiled=True).astype(jnp.float32)]
    all_to_all x2 -> x0, starting transfers between devices: 10 us -> none  [the longest x1 6.58 us: body(): lax.all_to_all(spans, 'leaf', 0, 0, tiled=True).astype(jnp.float32)]
  transfers between devices with their start and end apart: 10 -> 17, of which waited for: 10 -> 14; matrix products, arithmetic and copies ran while one was open for 1% -> 1% of each run, Pallas kernels for 0% -> 0%
where the time goes in v4:
time: 367 us; the launch traced here: 365 us
  blocking collectives  221 us (60%)
  waiting for transfers between devices  66.8 us (18%)
  starting transfers between devices  42.2 us (11%)
  matrix products  16.8 us (5%)
  local copies, waits for them, and re-layouts  11.9 us (3%)
  other arithmetic  5.34 us (1%)
    all_to_all x10, blocking collectives, gather_rows(): lax.all_to_all(copies, axis, 0, 0, tiled=True).reshape(-1, block.shape[-1])  133 us
    all_to_all x6, blocking collectives, scatter_sum(): pieces = lax.all_to_all(pieces, axis, 0, 0, tiled=True)  88.4 us
    all_to_all x4, waiting for transfers between devices, scatter_sum(): pieces = lax.all_to_all(pieces, axis, 0, 0, tiled=True)  31.9 us
    ppermute x4, waiting for transfers between devices, from_partner(): return lax.ppermute(block, axis, route)  16 us
    all_to_all x4, starting transfers between devices, scatter_sum(): pieces = lax.all_to_all(pieces, axis, 0, 0, tiled=True)  14.7 us
    ppermute x6, starting transfers between devices, leaf_exchange(): came.append(lax.ppermute(pick_span(blocks, group ^ step), 'leaf', route))  13.2 us
    dot_general x5, matrix products, forward_apply(): jnp.dot(matrix, gathered, preferred_element_type=jnp.float32)  11.6 us
    ppermute x3, waiting for transfers between devices, forward_apply(): total = total + lax.ppermute(sent, 'leaf', route).astype(jnp.float32)  10 us
  transfers between devices with their start and end apart: 17, of which 14 were waited for; matrix products, arithmetic and copies ran while one was open for 1% of the time, Pallas kernels for 0%

profile of v4, /device:TPU:2, one launch (start us, length us, event | category | flops | bytes accessed | tf_op | source)
XLA Modules:
  0.0 365.4 jit_solution(8328310870318797669)
XLA Ops:
  0.6 1.1 convert_bitcast_fusion
  1.7 15.7 %all_to_all.100 = bf16[8,128,256]{2,1,0:T(8,128)(2,1)S(1)} all-to-all(bf16[8,128,256]{2,1,0:T(8,128)(2,1)S(1)} %broadcast_in_dim.29), channel_id=1, replica_groups=mesh['leaf'=4,'row'=8,'col'=8] {'row'}, dimensions={0} | all-to-all | bytes 1048576 | tf_op jit(solution)/shard_map/all_to_all | solution.py:44
  17.4 2.3 fusion.10
  19.8 13.7 %all_to_all.101 = bf16[8,128,256]{2,1,0:T(8,128)(2,1)S(1)} all-to-all(bf16[8,128,256]{2,1,0:T(8,128)(2,1)S(1)} %bitcast.163), channel_id=1, replica_groups=mesh['leaf'=4,'row'=8,'col'=8] {'col'}, dimensions={0} | all-to-all | bytes 1048576 | tf_op jit(solution)/shard_map/all_to_all | solution.py:37
  33.5 12.8 %all_to_all.102 = bf16[8,128,256]{2,1,0:T(8,128)(2,1)S(1)} all-to-all(bf16[8,128,256]{2,1,0:T(8,128)(2,1)S(1)} %broadcast_in_dim.30), channel_id=1, replica_groups=mesh['leaf'=4,'row'=8,'col'=8] {'col'}, dimensions={0} | all-to-all | bytes 1048576 | tf_op jit(solution)/shard_map/all_to_all | solution.py:44
  46.3 0.7 fusion.25
  47.1 0.9 copy.87
  48.0 3.5 all-to-all-start.3
  51.5 9.4 %all-to-all-done.3 = bf16[8,128,256]{1,2,0:T(8,128)(2,1)S(1)} async-done(((bf16[8,128,256]{1,2,0:T(8,128)(2,1)}), bf16[8,128,256]{1,2,0:T(8,128)(2,1)S(1)}, u32[]{:S(2)}, u32[]{:S(2)}) %all-to-all-start.3) | async-done | bytes 524320 | tf_op jit(solution)/shard_map/all_to_all | solution.py:37
  61.1 3.4 collective-permute-start
  64.5 1.0 scatter_custom_fusion
  65.5 0.8 collective-permute-done
  66.3 1.0 scatter_custom_fusion.1
  67.4 11.1 %all_to_all.103 = bf16[8,96,256]{2,1,0:T(8,128)(2,1)S(1)} all-to-all(bf16[8,96,256]{2,1,0:T(8,128)(2,1)S(1)} %broadcast_in_dim.31), channel_id=1, replica_groups=mesh['leaf'=4,'row'=8,'col'=8] {'row'}, dimensions={0} | all-to-all | bytes 786432 | tf_op jit(solution)/shard_map/all_to_all | solution.py:44
  78.5 1.7 fusion.1
  80.2 1.4 copy.58
  81.6 15.6 %all_to_all.104 = bf16[8,192,256]{2,1,0:T(8,128)(2,1)S(1)} all-to-all(bf16[8,192,256]{2,1,0:T(8,128)(2,1)S(1)} %bitcast.149), channel_id=1, replica_groups=mesh['leaf'=4,'row'=8,'col'=8] {'col'}, dimensions={0} | all-to-all | bytes 1572864 | tf_op jit(solution)/shard_map/all_to_all | solution.py:37
  97.3 3.3 collective-permute-start.1
  100.6 4.5 %collective-permute-done.1 = bf16[192,256]{1,0:T(8,128)(2,1)S(1)} collective-permute-done((bf16[192,256]{1,0:T(8,128)(2,1)S(1)}, bf16[192,256]{1,0:T(8,128)(2,1)S(1)}, u32[]{:S(2)}, u32[]{:S(2)}) %collective-permute-start.1) | collective-permute-done | bytes 98336 | tf_op jit(solution)/shard_map/ppermute | solution.py:16
  105.2 15.6 %all_to_all.105 = bf16[8,192,256]{2,1,0:T(8,128)(2,1)S(1)} all-to-all(bf16[8,192,256]{2,1,0:T(8,128)(2,1)S(1)} %broadcast_in_dim.32), channel_id=1, replica_groups=mesh['leaf'=4,'row'=8,'col'=8] {'col'}, dimensions={0} | all-to-all | bytes 1572864 | tf_op jit(solution)/shard_map/all_to_all | solution.py:44
  121.4 0.8 copy.59
  122.3 3.4 all-to-all-start.7
  125.8 7.0 %all-to-all-done.7 = bf16[8,64,256]{2,1,0:T(8,128)(2,1)S(1)} async-done(((bf16[8,64,256]{2,1,0:T(8,128)(2,1)}), bf16[8,64,256]{2,1,0:T(8,128)(2,1)S(1)}, u32[]{:S(2)}, u32[]{:S(2)}) %all-to-all-start.7) | async-done | bytes 262176 | tf_op jit(solution)/shard_map/all_to_all | solution.py:37
  132.9 2.1 collective-permute-start.2
  135.0 4.5 %collective-permute-start.3 = (bf16[16,256]{1,0:T(8,128)(2,1)S(1)}, bf16[16,256]{1,0:T(8,128)(2,1)S(1)}, u32[]{:S(2)}, u32[]{:S(2)}) collective-permute-start(bf16[16,256]{1,0:T(8,128)(2,1)S(1)} %get-tuple-element.19), channel_id=1, source_target_pairs={{0,128},{64,192},{128,0},{192,64},{1,129},{65,193},{129,1},{193,65... | collective-permute-start | bytes 24584 | tf_op jit(solution)/shard_map/ppermute | solution.py:25
  139.5 3.0 collective-permute-done.3
  142.6 2.7 collective-permute-done.4
  145.9 1.0 scatter_custom_fusion.2
  147.0 9.8 %all_to_all.106 = bf16[8,64,256]{2,1,0:T(8,128)(2,1)S(1)} all-to-all(bf16[8,64,256]{2,1,0:T(8,128)(2,1)S(1)} %broadcast_in_dim.33), channel_id=1, replica_groups=mesh['leaf'=4,'row'=8,'col'=8] {'row'}, dimensions={0} | all-to-all | bytes 524288 | tf_op jit(solution)/shard_map/all_to_all | solution.py:44
  156.8 2.4 convolution_convert_fusion
  159.2 18.4 %all_to_all.107 = bf16[8,256,256]{1,2,0:T(8,128)(2,1)S(1)} all-to-all(bf16[8,256,256]{1,2,0:T(8,128)(2,1)S(1)} %bitcast.148), channel_id=1, replica_groups=mesh['leaf'=4,'row'=8,'col'=8] {'col'}, dimensions={0} | all-to-all | bytes 2097152 | tf_op jit(solution)/shard_map/all_to_all | solution.py:37
  177.8 1.8 collective-permute-start.5
  179.6 1.8 collective-permute-start.6
  181.4 3.0 collective-permute-start.7
  184.4 6.8 %collective-permute-done.5 = bf16[256,256]{0,1:T(8,128)(2,1)S(1)} collective-permute-done((bf16[256,256]{0,1:T(8,128)(2,1)S(1)}, bf16[256,256]{0,1:T(8,128)(2,1)S(1)}, u32[]{:S(2)}, u32[]{:S(2)}) %collective-permute-start.5) | collective-permute-done | bytes 131104 | tf_op jit(solution)/shard_map/ppermute | solution.py:60
  191.2 0.7 collective-permute-done.6
  192.0 2.5 collective-permute-done.7
  194.7 18.5 %all_to_all.108 = bf16[8,256,256]{2,1,0:T(8,128)(2,1)S(1)} all-to-all(bf16[8,256,256]{2,1,0:T(8,128)(2,1)S(1)} %broadcast_in_dim.34), channel_id=1, replica_groups=mesh['leaf'=4,'row'=8,'col'=8] {'col'}, dimensions={0} | all-to-all | bytes 2097152 | tf_op jit(solution)/shard_map/all_to_all | solution.py:44
  214.0 0.8 copy.63
  214.8 4.3 %all-to-all-start.11 = ((bf16[8,64,256]{2,1,0:T(8,128)(2,1)}), bf16[8,64,256]{2,1,0:T(8,128)(2,1)S(1)}, u32[]{:S(2)}, u32[]{:S(2)}) async-start(bf16[8,64,256]{2,1,0:T(8,128)(2,1)} %bitcast.38), calls=%async_computation.11 | async-start | bytes 524288 | tf_op jit(solution)/shard_map/all_to_all | solution.py:37
  219.1 7.2 %all-to-all-done.11 = bf16[8,64,256]{2,1,0:T(8,128)(2,1)S(1)} async-done(((bf16[8,64,256]{2,1,0:T(8,128)(2,1)}), bf16[8,64,256]{2,1,0:T(8,128)(2,1)S(1)}, u32[]{:S(2)}, u32[]{:S(2)}) %all-to-all-start.11) | async-done | bytes 262176 | tf_op jit(solution)/shard_map/all_to_all | solution.py:37
  227.1 2.1 collective-permute-start.8
  229.2 1.5 collective-permute-start.9
  230.7 3.0 collective-permute-start.10
  233.6 3.1 collective-permute-done.9
  238.0 9.8 %all_to_all.109 = bf16[8,64,256]{2,1,0:T(8,128)(2,1)S(1)} all-to-all(bf16[8,64,256]{2,1,0:T(8,128)(2,1)S(1)} %broadcast_in_dim.35), channel_id=1, replica_groups=mesh['leaf'=4,'row'=8,'col'=8] {'row'}, dimensions={0} | all-to-all | bytes 524288 | tf_op jit(solution)/shard_map/all_to_all | solution.py:44
  247.8 2.9 fusion
  250.7 1.4 copy.64
  252.2 15.7 %all_to_all.110 = bf16[8,192,256]{2,1,0:T(8,128)(2,1)S(1)} all-to-all(bf16[8,192,256]{2,1,0:T(8,128)(2,1)S(1)} %bitcast.150), channel_id=1, replica_groups=mesh['leaf'=4,'row'=8,'col'=8] {'col'}, dimensions={0} | all-to-all | bytes 1572864 | tf_op jit(solution)/shard_map/all_to_all | solution.py:37
  268.0 1.0 collective-permute-start.11
  269.0 6.3 %collective-permute-done.11 = bf16[192,256]{1,0:T(8,128)(2,1)S(1)} collective-permute-done((bf16[192,256]{1,0:T(8,128)(2,1)S(1)}, bf16[192,256]{1,0:T(8,128)(2,1)S(1)}, u32[]{:S(2)}, u32[]{:S(2)}) %collective-permute-start.11) | collective-permute-done | bytes 98336 | tf_op jit(solution)/shard_map/ppermute | solution.py:16
  275.3 15.6 %all_to_all.111 = bf16[8,192,256]{2,1,0:T(8,128)(2,1)S(1)} all-to-all(bf16[8,192,256]{2,1,0:T(8,128)(2,1)S(1)} %broadcast_in_dim.36), channel_id=1, replica_groups=mesh['leaf'=4,'row'=8,'col'=8] {'col'}, dimensions={0} | all-to-all | bytes 1572864 | tf_op jit(solution)/shard_map/all_to_all | solution.py:44
  290.9 0.8 fusion.31
  291.7 0.9 copy.65
  292.6 3.5 all-to-all-start.15
  296.1 8.3 %all-to-all-done.15 = bf16[8,96,256]{2,1,0:T(8,128)(2,1)S(1)} async-done(((bf16[8,96,256]{2,1,0:T(8,128)(2,1)}), bf16[8,96,256]{2,1,0:T(8,128)(2,1)S(1)}, u32[]{:S(2)}, u32[]{:S(2)}) %all-to-all-start.15) | async-done | bytes 393248 | tf_op jit(solution)/shard_map/all_to_all | solution.py:37
  306.0 4.4 %collective-permute-done.12 = bf16[64,256]{1,0:T(8,128)(2,1)S(1)} collective-permute-done((bf16[64,256]{1,0:T(8,128)(2,1)S(1)}, bf16[64,256]{1,0:T(8,128)(2,1)S(1)}, u32[]{:S(2)}, u32[]{:S(2)}) %collective-permute-start.12) | collective-permute-done | bytes 32800 | tf_op jit(solution)/shard_map/ppermute | solution.py:16
  310.5 11.1 %all_to_all.112 = bf16[8,128,256]{2,1,0:T(8,128)(2,1)S(1)} all-to-all(bf16[8,128,256]{2,1,0:T(8,128)(2,1)S(1)} %broadcast_in_dim.37), channel_id=1, replica_groups=mesh['leaf'=4,'row'=8,'col'=8] {'row'}, dimensions={0} | all-to-all | bytes 1048576 | tf_op jit(solution)/shard_map/all_to_all | solution.py:44
  321.6 2.4 fusion.22
  324.1 12.7 %all_to_all.113 = bf16[8,128,256]{1,2,0:T(8,128)(2,1)S(1)} all-to-all(bf16[8,128,256]{1,2,0:T(8,128)(2,1)S(1)} %bitcast.152), channel_id=1, replica_groups=mesh['leaf'=4,'row'=8,'col'=8] {'col'}, dimensions={0} | all-to-all | bytes 1048576 | tf_op jit(solution)/shard_map/all_to_all | solution.py:37
  337.0 12.8 %all_to_all.114 = bf16[8,128,256]{2,1,0:T(8,128)(2,1)S(1)} all-to-all(bf16[8,128,256]{2,1,0:T(8,128)(2,1)S(1)} %broadcast_in_dim.38), channel_id=1, replica_groups=mesh['leaf'=4,'row'=8,'col'=8] {'col'}, dimensions={0} | all-to-all | bytes 1048576 | tf_op jit(solution)/shard_map/all_to_all | solution.py:44
  349.8 2.3 fusion.28
  352.2 12.3 %all_to_all.115 = bf16[8,128,256]{1,2,0:T(8,128)(2,1)S(1)} all-to-all(bf16[8,128,256]{1,2,0:T(8,128)(2,1)S(1)} %bitcast.153), channel_id=1, replica_groups=mesh['leaf'=4,'row'=8,'col'=8] {'row'}, dimensions={0} | all-to-all | bytes 1048576 | tf_op jit(solution)/shard_map/all_to_all | solution.py:37
  364.6 0.8 copy.71
  (97 shorter events, 7.6 us)
Async XLA Ops:
  0.6 77.9 %copy-start = (bf16[1536,768]{1,0:T(8,128)(2,1)S(1)}, bf16[1536,768]{1,0:T(8,128)(2,1)}, u32[]{:S(2)}) copy-start(bf16[1536,768]{1,0:T(8,128)(2,1)} %param.17) | copy-start | bytes 7077892
  19.7 26.6 %copy-start.2 = (bf16[1,1024,1024]{2,1,0:T(8,128)(2,1)S(1)}, bf16[1,1024,1024]{2,1,0:T(8,128)(2,1)}, u32[]{:S(2)}) copy-start(bf16[1,1024,1024]{2,1,0:T(8,128)(2,1)} %param.16) | copy-start | bytes 6291460
  46.3 5.2 %copy-start.13 = (s32[1,1,1,2,64]{4,3,2,1,0:T(2,128)S(1)}, s32[1,1,1,2,64]{4,3,2,1,0:T(2,128)}, u32[]{:S(2)}) copy-start(s32[1,1,1,2,64]{4,3,2,1,0:T(2,128)} %param.20) | copy-start | bytes 1540
  47.1 17.4 %copy-start.11 = (f32[1,1,1,96,256]{4,3,2,1,0:T(8,128)S(1)}, f32[1,1,1,96,256]{4,3,2,1,0:T(8,128)}, u32[]{:S(2)}) copy-start(f32[1,1,1,96,256]{4,3,2,1,0:T(8,128)} %param.13) | copy-start | bytes 294916
  48.0 12.9 %all-to-all-start.3 = ((bf16[8,128,256]{1,2,0:T(8,128)(2,1)}), bf16[8,128,256]{1,2,0:T(8,128)(2,1)S(1)}, u32[]{:S(2)}, u32[]{:S(2)}) async-start(bf16[8,128,256]{1,2,0:T(8,128)(2,1)} %bitcast.146), calls=%async_computation.3 | async-start | bytes 1048576 | tf_op jit(solution)/shard_map/all_to_all | solution.py:37
  61.1 5.3 %collective-permute-start = (bf16[64,256]{1,0:T(8,128)(2,1)S(1)}, bf16[64,256]{1,0:T(8,128)(2,1)S(1)}, u32[]{:S(2)}, u32[]{:S(2)}) collective-permute-start(bf16[64,256]{1,0:T(8,128)(2,1)S(1)} %fusion.46), channel_id=1, source_target_pairs={{0,64},{64,0},{128,192},{192,128},{1,65},{65,1},{129,193},{193,129... | collective-permute-start | bytes 98312 | tf_op jit(solution)/shard_map/ppermute | solution.py:16
  97.2 23.6 %copy-start.1 = (bf16[1536,512]{1,0:T(8,128)(2,1)S(1)}, bf16[1536,512]{1,0:T(8,128)(2,1)}, u32[]{:S(2)}) copy-start(bf16[1536,512]{1,0:T(8,128)(2,1)} %param.18) | copy-start | bytes 4718596
  97.3 7.8 %collective-permute-start.1 = (bf16[192,256]{1,0:T(8,128)(2,1)S(1)}, bf16[192,256]{1,0:T(8,128)(2,1)S(1)}, u32[]{:S(2)}, u32[]{:S(2)}) collective-permute-start(bf16[192,256]{1,0:T(8,128)(2,1)S(1)} %convert_element_type.203), channel_id=1, source_target_pairs={{0,64},{64,0},{128,192},{192,128},{1,65},{65,1},{129,193},{193,129... | collective-permute-start | bytes 294920 | tf_op jit(solution)/shard_map/ppermute | solution.py:16
  105.1 15.7 %copy-start.5 = (bf16[192,256]{1,0:T(8,128)(2,1)}, bf16[192,256]{1,0:T(8,128)(2,1)S(1)}, u32[]{:S(2)}) copy-start(bf16[192,256]{1,0:T(8,128)(2,1)S(1)} %collective-permute-done.1) | copy-start | bytes 294916
  120.8 4.9 %copy-start.12 = (s32[1,1,1,4,16]{4,3,2,1,0:T(4,128)S(1)}, s32[1,1,1,4,16]{4,3,2,1,0:T(4,128)}, u32[]{:S(2)}) copy-start(s32[1,1,1,4,16]{4,3,2,1,0:T(4,128)} %param.21) | copy-start | bytes 772
  120.8 25.1 %copy-start.10 = (f32[1,1,1,64,256]{4,3,2,1,0:T(8,128)S(1)}, f32[1,1,1,64,256]{4,3,2,1,0:T(8,128)}, u32[]{:S(2)}) copy-start(f32[1,1,1,64,256]{4,3,2,1,0:T(8,128)} %param.14) | copy-start | bytes 196612
  122.3 10.6 %all-to-all-start.7 = ((bf16[8,64,256]{2,1,0:T(8,128)(2,1)}), bf16[8,64,256]{2,1,0:T(8,128)(2,1)S(1)}, u32[]{:S(2)}, u32[]{:S(2)}) async-start(bf16[8,64,256]{2,1,0:T(8,128)(2,1)} %bitcast.25), calls=%async_computation.7 | async-start | bytes 524288 | tf_op jit(solution)/shard_map/all_to_all | solution.py:37
  132.9 6.6 %collective-permute-start.2 = (bf16[16,256]{1,0:T(8,128)(2,1)S(1)}, bf16[16,256]{1,0:T(8,128)(2,1)S(1)}, u32[]{:S(2)}, u32[]{:S(2)}) collective-permute-start(bf16[16,256]{1,0:T(8,128)(2,1)S(1)} %get-tuple-element.20), channel_id=1, source_target_pairs={{0,64},{64,0},{128,192},{192,128},{1,65},{65,1},{129,193},{193,129... | collective-permute-start | bytes 24584 | tf_op jit(solution)/shard_map/ppermute | solution.py:25
  135.0 7.6 %collective-permute-start.3 = (bf16[16,256]{1,0:T(8,128)(2,1)S(1)}, bf16[16,256]{1,0:T(8,128)(2,1)S(1)}, u32[]{:S(2)}, u32[]{:S(2)}) collective-permute-start(bf16[16,256]{1,0:T(8,128)(2,1)S(1)} %get-tuple-element.19), channel_id=1, source_target_pairs={{0,128},{64,192},{128,0},{192,64},{1,129},{65,193},{129,1},{193,65... | collective-permute-start | bytes 24584 | tf_op jit(solution)/shard_map/ppermute | solution.py:25
  139.5 5.8 %collective-permute-start.4 = (bf16[16,256]{1,0:T(8,128)(2,1)S(1)}, bf16[16,256]{1,0:T(8,128)(2,1)S(1)}, u32[]{:S(2)}, u32[]{:S(2)}) collective-permute-start(bf16[16,256]{1,0:T(8,128)(2,1)S(1)} %get-tuple-element.18), channel_id=1, source_target_pairs={{0,192},{64,128},{128,64},{192,0},{1,193},{65,129},{129,65},{193,1... | collective-permute-start | bytes 24584 | tf_op jit(solution)/shard_map/ppermute | solution.py:25
  177.8 13.4 %collective-permute-start.5 = (bf16[256,256]{0,1:T(8,128)(2,1)S(1)}, bf16[256,256]{0,1:T(8,128)(2,1)S(1)}, u32[]{:S(2)}, u32[]{:S(2)}) collective-permute-start(bf16[256,256]{0,1:T(8,128)(2,1)S(1)} %convert_element_type.215), channel_id=1, source_target_pairs={{0,64},{64,0},{128,192},{192,128},{1,65},{65,1},{129,193},{193,129... | collective-permute-start | bytes 393224 | tf_op jit(solution)/shard_map/ppermute | solution.py:60
  179.6 12.4 %collective-permute-start.6 = (bf16[256,256]{0,1:T(8,128)(2,1)S(1)}, bf16[256,256]{0,1:T(8,128)(2,1)S(1)}, u32[]{:S(2)}, u32[]{:S(2)}) collective-permute-start(bf16[256,256]{0,1:T(8,128)(2,1)S(1)} %convert_element_type.215), channel_id=1, source_target_pairs={{0,128},{64,192},{128,0},{192,64},{1,129},{65,193},{129,1},{193,65... | collective-permute-start | bytes 393224 | tf_op jit(solution)/shard_map/ppermute | solution.py:60
  181.4 13.1 %collective-permute-start.7 = (bf16[256,256]{0,1:T(8,128)(2,1)S(1)}, bf16[256,256]{0,1:T(8,128)(2,1)S(1)}, u32[]{:S(2)}, u32[]{:S(2)}) collective-permute-start(bf16[256,256]{0,1:T(8,128)(2,1)S(1)} %convert_element_type.215), channel_id=1, source_target_pairs={{0,192},{64,128},{128,64},{192,0},{1,193},{65,129},{129,65},{193,1... | collective-permute-start | bytes 393224 | tf_op jit(solution)/shard_map/ppermute | solution.py:60
  194.6 18.6 %copy-start.3 = (bf16[2048,512]{1,0:T(8,128)(2,1)S(1)}, bf16[2048,512]{1,0:T(8,128)(2,1)}, u32[]{:S(2)}) copy-start(bf16[2048,512]{1,0:T(8,128)(2,1)} %param.19) | copy-start | bytes 6291460
  214.8 11.5 %all-to-all-start.11 = ((bf16[8,64,256]{2,1,0:T(8,128)(2,1)}), bf16[8,64,256]{2,1,0:T(8,128)(2,1)S(1)}, u32[]{:S(2)}, u32[]{:S(2)}) async-start(bf16[8,64,256]{2,1,0:T(8,128)(2,1)} %bitcast.38), calls=%async_computation.11 | async-start | bytes 524288 | tf_op jit(solution)/shard_map/all_to_all | solution.py:37
  226.4 25.8 %copy-start.4 = (f32[64,256]{1,0:T(8,128)}, f32[64,256]{1,0:T(8,128)S(1)}, u32[]{:S(2)}) copy-start(f32[64,256]{1,0:T(8,128)S(1)} %convert_reduce_fusion.8) | copy-start | bytes 196612
  227.1 6.6 %collective-permute-start.8 = (bf16[16,256]{1,0:T(8,128)(2,1)S(1)}, bf16[16,256]{1,0:T(8,128)(2,1)S(1)}, u32[]{:S(2)}, u32[]{:S(2)}) collective-permute-start(bf16[16,256]{1,0:T(8,128)(2,1)S(1)} %get-tuple-element.16), channel_id=1, source_target_pairs={{0,64},{64,0},{128,192},{192,128},{1,65},{65,1},{129,193},{193,129... | collective-permute-start | bytes 24584 | tf_op jit(solution)/shard_map/ppermute | solution.py:25
  229.2 7.6 %collective-permute-start.9 = (bf16[16,256]{1,0:T(8,128)(2,1)S(1)}, bf16[16,256]{1,0:T(8,128)(2,1)S(1)}, u32[]{:S(2)}, u32[]{:S(2)}) collective-permute-start(bf16[16,256]{1,0:T(8,128)(2,1)S(1)} %get-tuple-element.15), channel_id=1, source_target_pairs={{0,128},{64,192},{128,0},{192,64},{1,129},{65,193},{129,1},{193,65... | collective-permute-start | bytes 24584 | tf_op jit(solution)/shard_map/ppermute | solution.py:25
  230.7 6.1 %collective-permute-start.10 = (bf16[16,256]{1,0:T(8,128)(2,1)S(1)}, bf16[16,256]{1,0:T(8,128)(2,1)S(1)}, u32[]{:S(2)}, u32[]{:S(2)}) collective-permute-start(bf16[16,256]{1,0:T(8,128)(2,1)S(1)} %get-tuple-element.14), channel_id=1, source_target_pairs={{0,192},{64,128},{128,64},{192,0},{1,193},{65,129},{129,65},{193,1... | collective-permute-start | bytes 24584 | tf_op jit(solution)/shard_map/ppermute | solution.py:25
  237.4 0.6 copy-start.8
  252.2 23.1 %copy-start.6 = (bf16[192,256]{1,0:T(8,128)(2,1)S(1)}, bf16[192,256]{1,0:T(8,128)(2,1)}, u32[]{:S(2)}) copy-start(bf16[192,256]{1,0:T(8,128)(2,1)} %copy-done.5) | copy-start | bytes 294916
  268.0 7.3 %collective-permute-start.11 = (bf16[192,256]{1,0:T(8,128)(2,1)S(1)}, bf16[192,256]{1,0:T(8,128)(2,1)S(1)}, u32[]{:S(2)}, u32[]{:S(2)}) collective-permute-start(bf16[192,256]{1,0:T(8,128)(2,1)S(1)} %convert_element_type.228), channel_id=1, source_target_pairs={{0,64},{64,0},{128,192},{192,128},{1,65},{65,1},{129,193},{193,129... | collective-permute-start | bytes 294920 | tf_op jit(solution)/shard_map/ppermute | solution.py:16
  290.9 13.5 %copy-start.9 = (bf16[4,16,256]{2,1,0:T(8,128)(2,1)S(1)}, bf16[4,16,256]{2,1,0:T(8,128)(2,1)}, u32[]{:S(2)}) copy-start(bf16[4,16,256]{2,1,0:T(8,128)(2,1)} %copy-done.8) | copy-start | bytes 98308
  292.6 11.7 %all-to-all-start.15 = ((bf16[8,96,256]{2,1,0:T(8,128)(2,1)}), bf16[8,96,256]{2,1,0:T(8,128)(2,1)S(1)}, u32[]{:S(2)}, u32[]{:S(2)}) async-start(bf16[8,96,256]{2,1,0:T(8,128)(2,1)} %bitcast.52), calls=%async_computation.15 | async-start | bytes 786432 | tf_op jit(solution)/shard_map/all_to_all | solution.py:37
  304.5 19.5 %copy-start.7 = (f32[96,256]{1,0:T(8,128)}, f32[96,256]{1,0:T(8,128)S(1)}, u32[]{:S(2)}) copy-start(f32[96,256]{1,0:T(8,128)S(1)} %convert_reduce_fusion.7) | copy-start | bytes 294916
  305.2 5.3 %collective-permute-start.12 = (bf16[64,256]{1,0:T(8,128)(2,1)S(1)}, bf16[64,256]{1,0:T(8,128)(2,1)S(1)}, u32[]{:S(2)}, u32[]{:S(2)}) collective-permute-start(bf16[64,256]{1,0:T(8,128)(2,1)S(1)} %gather_fusion.2), channel_id=1, source_target_pairs={{0,64},{64,0},{128,192},{192,128},{1,65},{65,1},{129,193},{193,129... | collective-permute-start | bytes 98312 | tf_op jit(solution)/shard_map/ppermute | solution.py:16

commit v5 on v4

--- a/solution.py
+++ b/solution.py
@@ -19,12 +19,15 @@
 def leaf_exchange(blocks):
     group = lax.axis_index("leaf")
     count = lax.axis_size("leaf")
-    came = [pick_span(blocks, group)]
-    for step in range(1, count):
-        route = [(low, low ^ step) for low in range(count)]
-        came.append(lax.ppermute(pick_span(blocks, group ^ step), "leaf", route))
+    near = [(low, low ^ 1) for low in range(count)]
+    wrap = [(low, low ^ 3) for low in range(count)]
+    first = lax.ppermute(
+        jnp.stack([pick_span(blocks, group ^ 1), pick_span(blocks, group ^ 2)]), "leaf", near
+    )
+    second = lax.ppermute(jnp.stack([pick_span(blocks, group ^ 3), first[1]]), "leaf", wrap)
+    came = jnp.stack([pick_span(blocks, group), first[0], second[1], second[0]])
     order = jnp.bitwise_xor(jnp.arange(count, dtype=jnp.int32), group)
-    return jnp.take(jnp.stack(came), order, axis=0)
+    return jnp.take(came, order, axis=0)
 
 
 def partner(block_data, leaf_bit):
@@ -53,12 +56,9 @@
         result = result + partner(result, leaf_bits[0])
     elif leaf_bits:
         count = lax.axis_size("leaf")
-        sent = result.astype(jnp.bfloat16)
-        total = result
-        for step in range(1, count):
+        for step in (1, 3):
             route = [(low, low ^ step) for low in range(count)]
-            total = total + lax.ppermute(sent, "leaf", route).astype(jnp.float32)
-        result = total
+            result = result + lax.ppermute(result.astype(jnp.bfloat16), "leaf", route).astype(jnp.float32)
     return result
 
 

time: 367 us -> 367 us (level)
    ppermute x9 -> x6, starting transfers between devices: 19.8 us -> 16.6 us  [the longest x2 7.27 us: leaf_exchange(): lax.ppermute(jnp.stack([pick_span(blocks, group ^ 3), first[1]]), 'leaf',...]
    ppermute x9 -> x6, waiting for transfers between devices: 18.9 us -> 22 us  [the longest x2 12.3 us: forward_apply(): lax.ppermute(result.astype(jnp.bfloat16), 'leaf', route).astype(jnp.float32)]
  transfers between devices with their start and end apart: 17 -> 14, of which waited for: 14 -> 14; matrix products, arithmetic and copies ran while one was open for 1% -> 1% of each run, Pallas kernels for 0% -> 0%
where the time goes in v5:
time: 367 us; the launch traced here: 365 us
  blocking collectives  221 us (60%)
  waiting for transfers between devices  67.2 us (18%)
  starting transfers between devices  41.9 us (11%)
  matrix products  16.8 us (5%)
  local copies, waits for them, and re-layouts  11.9 us (3%)
  other arithmetic  5.37 us (1%)
    all_to_all x10, blocking collectives, gather_rows(): lax.all_to_all(copies, axis, 0, 0, tiled=True).reshape(-1, block.shape[-1])  132 us
    all_to_all x6, blocking collectives, scatter_sum(): pieces = lax.all_to_all(pieces, axis, 0, 0, tiled=True)  88.5 us
    all_to_all x4, waiting for transfers between devices, scatter_sum(): pieces = lax.all_to_all(pieces, axis, 0, 0, tiled=True)  31.9 us
    all_to_all x4, starting transfers between devices, scatter_sum(): pieces = lax.all_to_all(pieces, axis, 0, 0, tiled=True)  14.8 us
    ppermute x4, waiting for transfers between devices, from_partner(): return lax.ppermute(block, axis, route)  13.3 us
    ppermute x2, waiting for transfers between devices, forward_apply(): lax.ppermute(result.astype(jnp.bfloat16), 'leaf', route).astype(jnp.float32)  12.3 us
    dot_general x5, matrix products, forward_apply(): jnp.dot(matrix, gathered, preferred_element_type=jnp.float32)  11.6 us
    ppermute x4, starting transfers between devices, from_partner(): return lax.ppermute(block, axis, route)  10.5 us
  transfers between devices with their start and end apart: 14, of which 14 were waited for; matrix products, arithmetic and copies ran while one was open for 1% of the time, Pallas kernels for 0%

profile of v5, /device:TPU:2, one launch (start us, length us, event | category | flops | bytes accessed | tf_op | source)
XLA Modules:
  0.0 365.2 jit_solution(5751094089535307946)
XLA Ops:
  0.6 1.1 convert_bitcast_fusion
  1.7 15.7 %all_to_all.100 = bf16[8,128,256]{2,1,0:T(8,128)(2,1)S(1)} all-to-all(bf16[8,128,256]{2,1,0:T(8,128)(2,1)S(1)} %broadcast_in_dim.29), channel_id=1, replica_groups=mesh['leaf'=4,'row'=8,'col'=8] {'row'}, dimensions={0} | all-to-all | bytes 1048576 | tf_op jit(solution)/shard_map/all_to_all | solution.py:47
  17.4 2.3 fusion.10
  19.8 13.7 %all_to_all.101 = bf16[8,128,256]{2,1,0:T(8,128)(2,1)S(1)} all-to-all(bf16[8,128,256]{2,1,0:T(8,128)(2,1)S(1)} %bitcast.145), channel_id=1, replica_groups=mesh['leaf'=4,'row'=8,'col'=8] {'col'}, dimensions={0} | all-to-all | bytes 1048576 | tf_op jit(solution)/shard_map/all_to_all | solution.py:40
  33.5 12.8 %all_to_all.102 = bf16[8,128,256]{2,1,0:T(8,128)(2,1)S(1)} all-to-all(bf16[8,128,256]{2,1,0:T(8,128)(2,1)S(1)} %broadcast_in_dim.30), channel_id=1, replica_groups=mesh['leaf'=4,'row'=8,'col'=8] {'col'}, dimensions={0} | all-to-all | bytes 1048576 | tf_op jit(solution)/shard_map/all_to_all | solution.py:47
  46.3 0.7 fusion.25
  47.1 0.9 copy.87
  48.0 3.5 all-to-all-start.3
  51.5 9.4 %all-to-all-done.3 = bf16[8,128,256]{1,2,0:T(8,128)(2,1)S(1)} async-done(((bf16[8,128,256]{1,2,0:T(8,128)(2,1)}), bf16[8,128,256]{1,2,0:T(8,128)(2,1)S(1)}, u32[]{:S(2)}, u32[]{:S(2)}) %all-to-all-start.3) | async-done | bytes 524320 | tf_op jit(solution)/shard_map/all_to_all | solution.py:40
  61.1 3.4 collective-permute-start
  64.5 1.0 scatter_custom_fusion
  65.5 0.8 collective-permute-done
  66.3 1.0 scatter_custom_fusion.1
  67.4 11.1 %all_to_all.103 = bf16[8,96,256]{2,1,0:T(8,128)(2,1)S(1)} all-to-all(bf16[8,96,256]{2,1,0:T(8,128)(2,1)S(1)} %broadcast_in_dim.31), channel_id=1, replica_groups=mesh['leaf'=4,'row'=8,'col'=8] {'row'}, dimensions={0} | all-to-all | bytes 786432 | tf_op jit(solution)/shard_map/all_to_all | solution.py:47
  78.5 1.7 fusion.1
  80.2 1.4 copy.58
  81.6 15.6 %all_to_all.104 = bf16[8,192,256]{2,1,0:T(8,128)(2,1)S(1)} all-to-all(bf16[8,192,256]{2,1,0:T(8,128)(2,1)S(1)} %bitcast.131), channel_id=1, replica_groups=mesh['leaf'=4,'row'=8,'col'=8] {'col'}, dimensions={0} | all-to-all | bytes 1572864 | tf_op jit(solution)/shard_map/all_to_all | solution.py:40
  97.3 3.3 collective-permute-start.1
  100.6 4.5 %collective-permute-done.1 = bf16[192,256]{1,0:T(8,128)(2,1)S(1)} collective-permute-done((bf16[192,256]{1,0:T(8,128)(2,1)S(1)}, bf16[192,256]{1,0:T(8,128)(2,1)S(1)}, u32[]{:S(2)}, u32[]{:S(2)}) %collective-permute-start.1) | collective-permute-done | bytes 98336 | tf_op jit(solution)/shard_map/ppermute | solution.py:16
  105.2 15.6 %all_to_all.105 = bf16[8,192,256]{2,1,0:T(8,128)(2,1)S(1)} all-to-all(bf16[8,192,256]{2,1,0:T(8,128)(2,1)S(1)} %broadcast_in_dim.32), channel_id=1, replica_groups=mesh['leaf'=4,'row'=8,'col'=8] {'col'}, dimensions={0} | all-to-all | bytes 1572864 | tf_op jit(solution)/shard_map/all_to_all | solution.py:47
  121.4 0.8 copy.59
  122.3 3.4 all-to-all-start.7
  125.8 7.0 %all-to-all-done.7 = bf16[8,64,256]{2,1,0:T(8,128)(2,1)S(1)} async-done(((bf16[8,64,256]{2,1,0:T(8,128)(2,1)}), bf16[8,64,256]{2,1,0:T(8,128)(2,1)S(1)}, u32[]{:S(2)}, u32[]{:S(2)}) %all-to-all-start.7) | async-done | bytes 262176 | tf_op jit(solution)/shard_map/all_to_all | solution.py:40
  132.9 2.1 collective-permute-start.2
  135.1 2.8 collective-permute-done.2
  137.8 4.0 %collective-permute-start.3 = (bf16[2,16,256]{2,1,0:T(8,128)(2,1)S(1)}, bf16[2,16,256]{2,1,0:T(8,128)(2,1)S(1)}, u32[]{:S(2)}, u32[]{:S(2)}) collective-permute-start(bf16[2,16,256]{2,1,0:T(8,128)(2,1)S(1)} %pad_maximum_fusion.4), channel_id=1, source_target_pairs={{0,192},{64,128},{128,64},{192,0},{1,193},{65,129},{129,65},{193,1... | collective-permute-start | bytes 49160 | tf_op jit(solution)/shard_map/ppermute | solution.py:27
  141.8 1.9 collective-permute-done.3
  144.3 1.0 scatter_custom_fusion.2
  145.4 9.7 %all_to_all.106 = bf16[8,64,256]{2,1,0:T(8,128)(2,1)S(1)} all-to-all(bf16[8,64,256]{2,1,0:T(8,128)(2,1)S(1)} %broadcast_in_dim.33), channel_id=1, replica_groups=mesh['leaf'=4,'row'=8,'col'=8] {'row'}, dimensions={0} | all-to-all | bytes 524288 | tf_op jit(solution)/shard_map/all_to_all | solution.py:47
  155.0 2.4 convolution_convert_fusion
  157.5 18.4 %all_to_all.107 = bf16[8,256,256]{1,2,0:T(8,128)(2,1)S(1)} all-to-all(bf16[8,256,256]{1,2,0:T(8,128)(2,1)S(1)} %bitcast.130), channel_id=1, replica_groups=mesh['leaf'=4,'row'=8,'col'=8] {'col'}, dimensions={0} | all-to-all | bytes 2097152 | tf_op jit(solution)/shard_map/all_to_all | solution.py:40
  176.1 2.1 collective-permute-start.4
  178.2 6.6 %collective-permute-done.4 = bf16[256,256]{0,1:T(8,128)(2,1)S(1)} collective-permute-done((bf16[256,256]{0,1:T(8,128)(2,1)S(1)}, bf16[256,256]{0,1:T(8,128)(2,1)S(1)}, u32[]{:S(2)}, u32[]{:S(2)}) %collective-permute-start.4) | collective-permute-done | bytes 131104 | tf_op jit(solution)/shard_map/ppermute | solution.py:61
  184.8 2.6 collective-permute-start.5
  187.3 5.7 %collective-permute-done.5 = bf16[256,256]{0,1:T(8,128)(2,1)S(1)} collective-permute-done((bf16[256,256]{0,1:T(8,128)(2,1)S(1)}, bf16[256,256]{0,1:T(8,128)(2,1)S(1)}, u32[]{:S(2)}, u32[]{:S(2)}) %collective-permute-start.5) | collective-permute-done | bytes 131104 | tf_op jit(solution)/shard_map/ppermute | solution.py:61
  193.3 18.5 %all_to_all.108 = bf16[8,256,256]{2,1,0:T(8,128)(2,1)S(1)} all-to-all(bf16[8,256,256]{2,1,0:T(8,128)(2,1)S(1)} %broadcast_in_dim.34), channel_id=1, replica_groups=mesh['leaf'=4,'row'=8,'col'=8] {'col'}, dimensions={0} | all-to-all | bytes 2097152 | tf_op jit(solution)/shard_map/all_to_all | solution.py:47
  211.8 0.7 fusion.33
  212.5 0.8 copy.63
  213.4 4.5 %all-to-all-start.11 = ((bf16[8,64,256]{2,1,0:T(8,128)(2,1)}), bf16[8,64,256]{2,1,0:T(8,128)(2,1)S(1)}, u32[]{:S(2)}, u32[]{:S(2)}) async-start(bf16[8,64,256]{2,1,0:T(8,128)(2,1)} %bitcast.32), calls=%async_computation.11 | async-start | bytes 524288 | tf_op jit(solution)/shard_map/all_to_all | solution.py:40
  217.8 7.2 %all-to-all-done.11 = bf16[8,64,256]{2,1,0:T(8,128)(2,1)S(1)} async-done(((bf16[8,64,256]{2,1,0:T(8,128)(2,1)}), bf16[8,64,256]{2,1,0:T(8,128)(2,1)S(1)}, u32[]{:S(2)}, u32[]{:S(2)}) %all-to-all-start.11) | async-done | bytes 262176 | tf_op jit(solution)/shard_map/all_to_all | solution.py:40
  225.8 2.5 collective-permute-start.6
  228.3 2.5 collective-permute-done.6
  230.9 3.3 collective-permute-start.7
  234.2 2.6 collective-permute-done.7
  238.0 9.6 %all_to_all.109 = bf16[8,64,256]{2,1,0:T(8,128)(2,1)S(1)} all-to-all(bf16[8,64,256]{2,1,0:T(8,128)(2,1)S(1)} %broadcast_in_dim.35), channel_id=1, replica_groups=mesh['leaf'=4,'row'=8,'col'=8] {'row'}, dimensions={0} | all-to-all | bytes 524288 | tf_op jit(solution)/shard_map/all_to_all | solution.py:47
  247.7 2.9 fusion
  250.6 1.4 copy.64
  252.0 15.7 %all_to_all.110 = bf16[8,192,256]{2,1,0:T(8,128)(2,1)S(1)} all-to-all(bf16[8,192,256]{2,1,0:T(8,128)(2,1)S(1)} %bitcast.132), channel_id=1, replica_groups=mesh['leaf'=4,'row'=8,'col'=8] {'col'}, dimensions={0} | all-to-all | bytes 1572864 | tf_op jit(solution)/shard_map/all_to_all | solution.py:40
  267.8 2.4 collective-permute-start.8
  270.2 4.9 %collective-permute-done.8 = bf16[192,256]{1,0:T(8,128)(2,1)S(1)} collective-permute-done((bf16[192,256]{1,0:T(8,128)(2,1)S(1)}, bf16[192,256]{1,0:T(8,128)(2,1)S(1)}, u32[]{:S(2)}, u32[]{:S(2)}) %collective-permute-start.8) | collective-permute-done | bytes 98336 | tf_op jit(solution)/shard_map/ppermute | solution.py:16
  275.2 15.6 %all_to_all.111 = bf16[8,192,256]{2,1,0:T(8,128)(2,1)S(1)} all-to-all(bf16[8,192,256]{2,1,0:T(8,128)(2,1)S(1)} %broadcast_in_dim.36), channel_id=1, replica_groups=mesh['leaf'=4,'row'=8,'col'=8] {'col'}, dimensions={0} | all-to-all | bytes 1572864 | tf_op jit(solution)/shard_map/all_to_all | solution.py:47
  290.8 0.8 fusion.31
  291.6 0.9 copy.65
  292.5 3.5 all-to-all-start.15
  296.0 8.3 %all-to-all-done.15 = bf16[8,96,256]{2,1,0:T(8,128)(2,1)S(1)} async-done(((bf16[8,96,256]{2,1,0:T(8,128)(2,1)}), bf16[8,96,256]{2,1,0:T(8,128)(2,1)S(1)}, u32[]{:S(2)}, u32[]{:S(2)}) %all-to-all-start.15) | async-done | bytes 393248 | tf_op jit(solution)/shard_map/all_to_all | solution.py:40
  305.0 1.5 collective-permute-start.9
  307.2 3.1 collective-permute-done.9
  310.4 11.1 %all_to_all.112 = bf16[8,128,256]{2,1,0:T(8,128)(2,1)S(1)} all-to-all(bf16[8,128,256]{2,1,0:T(8,128)(2,1)S(1)} %broadcast_in_dim.37), channel_id=1, replica_groups=mesh['leaf'=4,'row'=8,'col'=8] {'row'}, dimensions={0} | all-to-all | bytes 1048576 | tf_op jit(solution)/shard_map/all_to_all | solution.py:47
  321.4 2.4 fusion.22
  323.9 12.7 %all_to_all.113 = bf16[8,128,256]{1,2,0:T(8,128)(2,1)S(1)} all-to-all(bf16[8,128,256]{1,2,0:T(8,128)(2,1)S(1)} %bitcast.134), channel_id=1, replica_groups=mesh['leaf'=4,'row'=8,'col'=8] {'col'}, dimensions={0} | all-to-all | bytes 1048576 | tf_op jit(solution)/shard_map/all_to_all | solution.py:40
  336.9 12.8 %all_to_all.114 = bf16[8,128,256]{2,1,0:T(8,128)(2,1)S(1)} all-to-all(bf16[8,128,256]{2,1,0:T(8,128)(2,1)S(1)} %broadcast_in_dim.38), channel_id=1, replica_groups=mesh['leaf'=4,'row'=8,'col'=8] {'col'}, dimensions={0} | all-to-all | bytes 1048576 | tf_op jit(solution)/shard_map/all_to_all | solution.py:47
  349.6 2.3 fusion.28
  352.1 12.4 %all_to_all.115 = bf16[8,128,256]{1,2,0:T(8,128)(2,1)S(1)} all-to-all(bf16[8,128,256]{1,2,0:T(8,128)(2,1)S(1)} %bitcast.135), channel_id=1, replica_groups=mesh['leaf'=4,'row'=8,'col'=8] {'row'}, dimensions={0} | all-to-all | bytes 1048576 | tf_op jit(solution)/shard_map/all_to_all | solution.py:40
  364.5 0.8 copy.71
  (100 shorter events, 6.8 us)
Async XLA Ops:
  0.6 77.9 %copy-start = (bf16[1536,768]{1,0:T(8,128)(2,1)S(1)}, bf16[1536,768]{1,0:T(8,128)(2,1)}, u32[]{:S(2)}) copy-start(bf16[1536,768]{1,0:T(8,128)(2,1)} %param.17) | copy-start | bytes 7077892
  19.7 26.6 %copy-start.2 = (bf16[1,1024,1024]{2,1,0:T(8,128)(2,1)S(1)}, bf16[1,1024,1024]{2,1,0:T(8,128)(2,1)}, u32[]{:S(2)}) copy-start(bf16[1,1024,1024]{2,1,0:T(8,128)(2,1)} %param.16) | copy-start | bytes 6291460
  46.3 5.2 %copy-start.13 = (s32[1,1,1,2,64]{4,3,2,1,0:T(2,128)S(1)}, s32[1,1,1,2,64]{4,3,2,1,0:T(2,128)}, u32[]{:S(2)}) copy-start(s32[1,1,1,2,64]{4,3,2,1,0:T(2,128)} %param.20) | copy-start | bytes 1540
  47.1 17.4 %copy-start.11 = (f32[1,1,1,96,256]{4,3,2,1,0:T(8,128)S(1)}, f32[1,1,1,96,256]{4,3,2,1,0:T(8,128)}, u32[]{:S(2)}) copy-start(f32[1,1,1,96,256]{4,3,2,1,0:T(8,128)} %param.13) | copy-start | bytes 294916
  48.0 12.9 %all-to-all-start.3 = ((bf16[8,128,256]{1,2,0:T(8,128)(2,1)}), bf16[8,128,256]{1,2,0:T(8,128)(2,1)S(1)}, u32[]{:S(2)}, u32[]{:S(2)}) async-start(bf16[8,128,256]{1,2,0:T(8,128)(2,1)} %bitcast.128), calls=%async_computation.3 | async-start | bytes 1048576 | tf_op jit(solution)/shard_map/all_to_all | solution.py:40
  61.1 5.3 %collective-permute-start = (bf16[64,256]{1,0:T(8,128)(2,1)S(1)}, bf16[64,256]{1,0:T(8,128)(2,1)S(1)}, u32[]{:S(2)}, u32[]{:S(2)}) collective-permute-start(bf16[64,256]{1,0:T(8,128)(2,1)S(1)} %fusion.47), channel_id=1, source_target_pairs={{0,64},{64,0},{128,192},{192,128},{1,65},{65,1},{129,193},{193,129... | collective-permute-start | bytes 98312 | tf_op jit(solution)/shard_map/ppermute | solution.py:16
  97.2 23.6 %copy-start.1 = (bf16[1536,512]{1,0:T(8,128)(2,1)S(1)}, bf16[1536,512]{1,0:T(8,128)(2,1)}, u32[]{:S(2)}) copy-start(bf16[1536,512]{1,0:T(8,128)(2,1)} %param.18) | copy-start | bytes 4718596
  97.3 7.8 %collective-permute-start.1 = (bf16[192,256]{1,0:T(8,128)(2,1)S(1)}, bf16[192,256]{1,0:T(8,128)(2,1)S(1)}, u32[]{:S(2)}, u32[]{:S(2)}) collective-permute-start(bf16[192,256]{1,0:T(8,128)(2,1)S(1)} %convert_element_type.203), channel_id=1, source_target_pairs={{0,64},{64,0},{128,192},{192,128},{1,65},{65,1},{129,193},{193,129... | collective-permute-start | bytes 294920 | tf_op jit(solution)/shard_map/ppermute | solution.py:16
  105.2 15.7 %copy-start.5 = (bf16[192,256]{1,0:T(8,128)(2,1)}, bf16[192,256]{1,0:T(8,128)(2,1)S(1)}, u32[]{:S(2)}) copy-start(bf16[192,256]{1,0:T(8,128)(2,1)S(1)} %collective-permute-done.1) | copy-start | bytes 294916
  120.8 4.9 %copy-start.12 = (s32[1,1,1,4,16]{4,3,2,1,0:T(4,128)S(1)}, s32[1,1,1,4,16]{4,3,2,1,0:T(4,128)}, u32[]{:S(2)}) copy-start(s32[1,1,1,4,16]{4,3,2,1,0:T(4,128)} %param.21) | copy-start | bytes 772
  120.8 23.5 %copy-start.10 = (f32[1,1,1,64,256]{4,3,2,1,0:T(8,128)S(1)}, f32[1,1,1,64,256]{4,3,2,1,0:T(8,128)}, u32[]{:S(2)}) copy-start(f32[1,1,1,64,256]{4,3,2,1,0:T(8,128)} %param.14) | copy-start | bytes 196612
  122.3 10.6 %all-to-all-start.7 = ((bf16[8,64,256]{2,1,0:T(8,128)(2,1)}), bf16[8,64,256]{2,1,0:T(8,128)(2,1)S(1)}, u32[]{:S(2)}, u32[]{:S(2)}) async-start(bf16[8,64,256]{2,1,0:T(8,128)(2,1)} %bitcast.25), calls=%async_computation.7 | async-start | bytes 524288 | tf_op jit(solution)/shard_map/all_to_all | solution.py:40
  132.9 4.9 %collective-permute-start.2 = (bf16[2,16,256]{2,1,0:T(8,128)(2,1)S(1)}, bf16[2,16,256]{2,1,0:T(8,128)(2,1)S(1)}, u32[]{:S(2)}, u32[]{:S(2)}) collective-permute-start(bf16[2,16,256]{2,1,0:T(8,128)(2,1)S(1)} %pad_maximum_fusion.3), channel_id=1, source_target_pairs={{0,64},{64,0},{128,192},{192,128},{1,65},{65,1},{129,193},{193,129... | collective-permute-start | bytes 49160 | tf_op jit(solution)/shard_map/ppermute | solution.py:24
  137.8 5.8 %collective-permute-start.3 = (bf16[2,16,256]{2,1,0:T(8,128)(2,1)S(1)}, bf16[2,16,256]{2,1,0:T(8,128)(2,1)S(1)}, u32[]{:S(2)}, u32[]{:S(2)}) collective-permute-start(bf16[2,16,256]{2,1,0:T(8,128)(2,1)S(1)} %pad_maximum_fusion.4), channel_id=1, source_target_pairs={{0,192},{64,128},{128,64},{192,0},{1,193},{65,129},{129,65},{193,1... | collective-permute-start | bytes 49160 | tf_op jit(solution)/shard_map/ppermute | solution.py:27
  176.1 8.7 %collective-permute-start.4 = (bf16[256,256]{0,1:T(8,128)(2,1)S(1)}, bf16[256,256]{0,1:T(8,128)(2,1)S(1)}, u32[]{:S(2)}, u32[]{:S(2)}) collective-permute-start(bf16[256,256]{0,1:T(8,128)(2,1)S(1)} %convert_element_type.215), channel_id=1, source_target_pairs={{0,64},{64,0},{128,192},{192,128},{1,65},{65,1},{129,193},{193,129... | collective-permute-start | bytes 393224 | tf_op jit(solution)/shard_map/ppermute | solution.py:61
  184.8 8.2 %collective-permute-start.5 = (bf16[256,256]{0,1:T(8,128)(2,1)S(1)}, bf16[256,256]{0,1:T(8,128)(2,1)S(1)}, u32[]{:S(2)}, u32[]{:S(2)}) collective-permute-start(bf16[256,256]{0,1:T(8,128)(2,1)S(1)} %fusion.34), channel_id=1, source_target_pairs={{0,192},{64,128},{128,64},{192,0},{1,193},{65,129},{129,65},{193,1... | collective-permute-start | bytes 393224 | tf_op jit(solution)/shard_map/ppermute | solution.py:61
  193.2 18.6 %copy-start.3 = (bf16[2048,512]{1,0:T(8,128)(2,1)S(1)}, bf16[2048,512]{1,0:T(8,128)(2,1)}, u32[]{:S(2)}) copy-start(bf16[2048,512]{1,0:T(8,128)(2,1)} %param.19) | copy-start | bytes 6291460
  213.4 11.7 %all-to-all-start.11 = ((bf16[8,64,256]{2,1,0:T(8,128)(2,1)}), bf16[8,64,256]{2,1,0:T(8,128)(2,1)S(1)}, u32[]{:S(2)}, u32[]{:S(2)}) async-start(bf16[8,64,256]{2,1,0:T(8,128)(2,1)} %bitcast.32), calls=%async_computation.11 | async-start | bytes 524288 | tf_op jit(solution)/shard_map/all_to_all | solution.py:40
  225.1 26.9 %copy-start.4 = (f32[64,256]{1,0:T(8,128)}, f32[64,256]{1,0:T(8,128)S(1)}, u32[]{:S(2)}) copy-start(f32[64,256]{1,0:T(8,128)S(1)} %convert_reduce_fusion.8) | copy-start | bytes 196612
  225.8 5.1 %collective-permute-start.6 = (bf16[2,16,256]{2,1,0:T(8,128)(2,1)S(1)}, bf16[2,16,256]{2,1,0:T(8,128)(2,1)S(1)}, u32[]{:S(2)}, u32[]{:S(2)}) collective-permute-start(bf16[2,16,256]{2,1,0:T(8,128)(2,1)S(1)} %pad_maximum_fusion.5), channel_id=1, source_target_pairs={{0,64},{64,0},{128,192},{192,128},{1,65},{65,1},{129,193},{193,129... | collective-permute-start | bytes 49160 | tf_op jit(solution)/shard_map/ppermute | solution.py:24
  230.9 5.8 %collective-permute-start.7 = (bf16[2,16,256]{2,1,0:T(8,128)(2,1)S(1)}, bf16[2,16,256]{2,1,0:T(8,128)(2,1)S(1)}, u32[]{:S(2)}, u32[]{:S(2)}) collective-permute-start(bf16[2,16,256]{2,1,0:T(8,128)(2,1)S(1)} %pad_maximum_fusion.6), channel_id=1, source_target_pairs={{0,192},{64,128},{128,64},{192,0},{1,193},{65,129},{129,65},{193,1... | collective-permute-start | bytes 49160 | tf_op jit(solution)/shard_map/ppermute | solution.py:27
  237.4 0.6 copy-start.8
  252.0 23.1 %copy-start.6 = (bf16[192,256]{1,0:T(8,128)(2,1)S(1)}, bf16[192,256]{1,0:T(8,128)(2,1)}, u32[]{:S(2)}) copy-start(bf16[192,256]{1,0:T(8,128)(2,1)} %copy-done.5) | copy-start | bytes 294916
  267.8 7.3 %collective-permute-start.8 = (bf16[192,256]{1,0:T(8,128)(2,1)S(1)}, bf16[192,256]{1,0:T(8,128)(2,1)S(1)}, u32[]{:S(2)}, u32[]{:S(2)}) collective-permute-start(bf16[192,256]{1,0:T(8,128)(2,1)S(1)} %convert_element_type.228), channel_id=1, source_target_pairs={{0,64},{64,0},{128,192},{192,128},{1,65},{65,1},{129,193},{193,129... | collective-permute-start | bytes 294920 | tf_op jit(solution)/shard_map/ppermute | solution.py:16
  290.8 13.5 %copy-start.9 = (bf16[4,16,256]{2,1,0:T(8,128)(2,1)S(1)}, bf16[4,16,256]{2,1,0:T(8,128)(2,1)}, u32[]{:S(2)}) copy-start(bf16[4,16,256]{2,1,0:T(8,128)(2,1)} %copy-done.8) | copy-start | bytes 98308
  292.5 11.7 %all-to-all-start.15 = ((bf16[8,96,256]{2,1,0:T(8,128)(2,1)}), bf16[8,96,256]{2,1,0:T(8,128)(2,1)S(1)}, u32[]{:S(2)}, u32[]{:S(2)}) async-start(bf16[8,96,256]{2,1,0:T(8,128)(2,1)} %bitcast.40), calls=%async_computation.15 | async-start | bytes 786432 | tf_op jit(solution)/shard_map/all_to_all | solution.py:40
  304.3 19.5 %copy-start.7 = (f32[96,256]{1,0:T(8,128)}, f32[96,256]{1,0:T(8,128)S(1)}, u32[]{:S(2)}) copy-start(f32[96,256]{1,0:T(8,128)S(1)} %convert_reduce_fusion.7) | copy-start | bytes 294916
  305.0 5.3 %collective-permute-start.9 = (bf16[64,256]{1,0:T(8,128)(2,1)S(1)}, bf16[64,256]{1,0:T(8,128)(2,1)S(1)}, u32[]{:S(2)}, u32[]{:S(2)}) collective-permute-start(bf16[64,256]{1,0:T(8,128)(2,1)S(1)} %gather_fusion.2), channel_id=1, source_target_pairs={{0,64},{64,0},{128,192},{192,128},{1,65},{65,1},{129,193},{193,129... | collective-permute-start | bytes 98312 | tf_op jit(solution)/shard_map/ppermute | solution.py:16
